TPU v7x, 768 devices: a whole 4x8x12 slice. The times are simulated.
768 devices in a mesh: chan: 12 (over z), tile: 64 (over x, y, core).
Axes of the slice: x: 4, y: 8, z: 12, core: 2. Of those that a mesh axis runs over, the one named last changes fastest.
Arguments:
- samples: float32 [64, 48, 12, 2, 128], P('tile', 'chan'), may hold values from -6 to 6
- uv_coords: float32 [64, 48, 12, 2, 128], P('tile', 'chan'), may hold values from 4 to 28
- block_owner: int32 [64, 48, 1], P('tile', 'chan'), may hold values from 0 to 63; in each aligned block of 48 rows (0 to 47, 48 to 95, ..., all dimensions but the last counted through in order) at most 2 rows name the same one
- placement_map: int32 [64, 48, 2], P('tile', 'chan'), may hold values from 0 to 2016, as said below
- block_count: int32 [64, 12], P('tile', 'chan'), may hold values from 2 to 4, as said below
Outputs:
- dirty_image: float32 [12, 2048, 2048], P('chan', 'tile')
Inputs may be any that keep to these rules, and one draw needn't show every extreme that they name: `block_owner`: in each row of 48 blocks (one tile index), no owner is named by more than 2 blocks, a bound that some block reaches. `placement_map`: component 0 is at most 0, component 1 at most 2016; that column is reached in every draw. `block_count`: some device holds 4 blocks with data in every draw.
All inputs are finite; a program needn't handle non-finite values.
Results may differ from a plain program's by a relative error of at most 0.0029.
Values may be sent and summed in bfloat16 or wider, within the bound.
No kernel may reach another device: no remote copies, remote signals or barrier semaphores. Data moves between devices by JAX's collectives and lax.ppermute only.
A program may use at most 32 MiB of HBM per device.

v0:
```python
import math

import jax
import jax.numpy as jnp
from jax import lax
from jax.sharding import PartitionSpec as P

G = 2048
NS = 32
META = 128
HIGH = lax.Precision.HIGH
HIGHEST = lax.Precision.HIGHEST


def phase_table(row_count, col_count, length, sign):
    index = jnp.arange(row_count)[:, None] * jnp.arange(col_count)[None, :] % length
    angle = sign * 2.0 * math.pi / length * index.astype(jnp.float32)
    return (jnp.cos(angle), jnp.sin(angle))


def block_matrix(real, imag):
    return jnp.stack([jnp.stack([real, -imag]), jnp.stack([imag, real])])


def offset_phase(coord):
    factor = 2.0 * math.pi / NS
    coarse = (8.0 * jnp.arange(4) - NS / 2.0).astype(jnp.float32)
    fine = jnp.arange(8).astype(jnp.float32)
    angle_c = coord[..., None] * coarse * factor
    angle_f = coord[..., None] * fine * factor
    cos_c, sin_c = jnp.cos(angle_c)[..., :, None], jnp.sin(angle_c)[..., :, None]
    cos_f, sin_f = jnp.cos(angle_f)[..., None, :], jnp.sin(angle_f)[..., None, :]
    real = cos_c * cos_f - sin_c * sin_f
    imag = sin_c * cos_f + cos_c * sin_f
    shape = coord.shape + (NS,)
    return real.reshape(shape), imag.reshape(shape)


def form_subgrids(masked, coords):
    count = masked.shape[0]
    cos_u, sin_u = offset_phase(coords[:, 0])
    cos_v, sin_v = offset_phase(coords[:, 1])
    vis_real = masked[:, 0, :, None]
    vis_imag = masked[:, 1, :, None]
    weight_real = vis_real * cos_u - vis_imag * sin_u
    weight_imag = vis_real * sin_u + vis_imag * cos_u
    left = jnp.concatenate([weight_real, weight_imag], axis=1)
    right = jnp.concatenate(
        [jnp.concatenate([cos_v, sin_v], axis=2), jnp.concatenate([-sin_v, cos_v], axis=2)], axis=1
    )
    image = jnp.einsum("ikx,iky->ixy", left, right, precision=HIGH)
    image = image.reshape(count, NS, 2, NS)
    table = block_matrix(*phase_table(NS, NS, NS, -1.0))
    half = jnp.einsum("ixcy,ocyq->ixoq", image, table, precision=HIGHEST)
    full = jnp.einsum("ocpx,ixcq->iopq", table, half, precision=HIGHEST)
    return (full / (NS * NS)).astype(jnp.bfloat16)


def slot_targets(owners, tile_count, capacity):
    onehot = (owners[:, None] == jnp.arange(tile_count)[None, :]).astype(jnp.int32)
    before = jnp.cumsum(onehot, axis=0) - onehot
    slot_rank = jnp.sum(before * onehot, axis=1)
    return owners * capacity + slot_rank


def place_windows(windows, col_hi, col_lo, col_blocks):
    slots = windows.shape[0]
    wide = jnp.arange(2 * NS)
    shift = (wide[None, None, :] == col_lo[:, None, None] + jnp.arange(NS)[None, :, None])
    shifted = jnp.einsum(
        "scpq,sqw->scpw", windows, shift.astype(jnp.bfloat16), preferred_element_type=jnp.float32
    ).astype(jnp.bfloat16)
    shifted = shifted.reshape(slots, 2, NS, 2, NS)
    hit = jnp.arange(col_blocks)[:, None, None] == col_hi[None, :, None] + jnp.arange(2)[None, None, :]
    grid = jnp.einsum(
        "bsk,scpka->cpba", hit.astype(jnp.bfloat16), shifted, preferred_element_type=jnp.float32
    )
    return grid.reshape(2, NS, col_blocks * NS)


def factor_lengths(length):
    outer_len = 2 ** ((length.bit_length() - 1) // 2)
    return (outer_len, length // outer_len)


def transform_rows(grid):
    rows = grid.shape[1]
    outer_len, inner_len = factor_lengths(G)
    split = grid.reshape(2, rows, inner_len, outer_len)
    first = block_matrix(*phase_table(inner_len, inner_len, inner_len, 1.0))
    section = jnp.einsum("opba,Pobc->Pcpa", split, first, precision=HIGH)
    twiddle_real, twiddle_imag = phase_table(inner_len, outer_len, G, 1.0)
    twiddle_real = twiddle_real[:, None, :]
    twiddle_imag = twiddle_imag[:, None, :]
    turned_real = section[0] * twiddle_real - section[1] * twiddle_imag
    turned_imag = section[0] * twiddle_imag + section[1] * twiddle_real
    turned = jnp.stack([turned_real, turned_imag])
    second = block_matrix(*phase_table(outer_len, outer_len, outer_len, 1.0))
    return jnp.einsum("Ocpa,POad->dcPp", turned, second, precision=HIGH)


def transform_cols(turned):
    outer_len, inner_len = factor_lengths(G)
    first = block_matrix(*phase_table(inner_len, inner_len, inner_len, 1.0))
    section = jnp.einsum("bmoa,Pobc->Pcma", turned, first, precision=HIGH)
    twiddle_real, twiddle_imag = phase_table(inner_len, outer_len, G, 1.0)
    twiddle_real = twiddle_real[:, None, :]
    twiddle_imag = twiddle_imag[:, None, :]
    turned_real = section[0] * twiddle_real - section[1] * twiddle_imag
    turned_imag = section[0] * twiddle_imag + section[1] * twiddle_real
    second_real, second_imag = phase_table(outer_len, outer_len, outer_len, 1.0)
    second = jnp.stack([second_real, -second_imag])
    stacked = jnp.stack([turned_real, turned_imag])
    final = jnp.einsum("ocma,oad->mdc", stacked, second, precision=HIGH)
    return final.reshape(final.shape[0], G)


def per_device(samples, uv_coords, block_owner, placement_map, block_count):
    chan_count = lax.axis_size("chan")
    tile_count = lax.axis_size("tile")
    blocks = samples.shape[1]
    channels = samples.shape[2]
    steps_time = samples.shape[-1]
    group_blocks = blocks * chan_count
    capacity = max(2, 2 * group_blocks // tile_count)
    band_rows = G // tile_count
    live_mask = (jnp.arange(blocks) < block_count.reshape(())).astype(jnp.float32)
    masked = samples[0] * live_mask[:, None, None, None]
    item_count = blocks * channels
    formed = form_subgrids(
        masked.reshape(item_count, 2, steps_time), uv_coords[0].reshape(item_count, 2, steps_time)
    )
    cell_count = 2 * NS * NS
    formed = formed.reshape(blocks, channels, cell_count)
    owners = block_owner[0, :, 0]
    cols = placement_map[0, :, 1]
    meta = jnp.stack([owners, cols // NS, cols % NS], axis=1).astype(jnp.bfloat16)
    meta = jnp.pad(meta, ((0, 0), (0, META - 3)))
    meta = jnp.broadcast_to(meta[:, None, :], (blocks, channels, META))
    payload = jnp.concatenate([formed, meta], axis=2)
    arrived = lax.all_to_all(payload, "chan", split_axis=1, concat_axis=0, tiled=True)
    arrived = arrived.reshape(group_blocks, cell_count + META)
    group_owners = arrived[:, cell_count].astype(jnp.int32)
    target = slot_targets(group_owners, tile_count, capacity)
    slot_count = tile_count * capacity
    pick = (jnp.arange(slot_count)[:, None] == target[None, :]).astype(jnp.bfloat16)
    outgoing = jnp.dot(pick, arrived, preferred_element_type=jnp.float32).astype(jnp.bfloat16)
    incoming = lax.all_to_all(outgoing, "tile", split_axis=0, concat_axis=0, tiled=True)
    windows = incoming[:, :cell_count].reshape(slot_count, 2, NS, NS)
    col_hi = incoming[:, cell_count + 1].astype(jnp.int32)
    col_lo = incoming[:, cell_count + 2].astype(jnp.int32)
    tile_grid = place_windows(windows, col_hi, col_lo, G // NS)
    half = transform_rows(tile_grid)
    half = half.reshape(tile_count, G // tile_count, 2, band_rows)
    turned = lax.all_to_all(half, "tile", split_axis=0, concat_axis=0, tiled=True)
    dirty_image = transform_cols(turned) / G
    return dirty_image[None]


def solution(mesh):
    in_specs = (
        P("tile", "chan", None, None, None),
        P("tile", "chan", None, None, None),
        P("tile", "chan", None),
        P("tile", "chan", None),
        P("tile", "chan"),
    )
    out_specs = P("chan", "tile", None)
    return jax.shard_map(
        per_device, mesh=mesh, in_specs=in_specs, out_specs=out_specs, check_vma=False
    )
```

profile of v0, /device:TPU:1, one launch (start us, length us, event | category | flops | bytes accessed | tf_op | source)
XLA Modules:
  0.0 119.7 jit_solution(10191097148634166490)
XLA Ops:
  0.0 0.1 multiply_sine_fusion
  0.1 0.1 fusion.73
  0.2 0.9 fusion.84
  1.1 1.5 %fusion.35 = (f32[48,128,8]{1,2,0:T(8,128)S(1)}, f32[48,128,8]{1,2,0:T(8,128)S(1)}, f32[48,128,8]{1,2,0:T(8,128)S(1)}, f32[48,128,8]{1,2,0:T(8,128)S(1)}) fusion(f32[8]{0:T(128)S(1)} %iota_convert_fusion, f32[48,128]{1,0:T(8,128)S(1)} %bitcast.166, f32[48,128]{1,0:T(8,128)S(1)} %bitcast.168), kind=kLoop, calls=%fused_computation.57 | loop fusion | flops 196608 | bytes 835616 | tf_op jit(solution)/shard_map/cos | solution.py:32
  2.6 1.6 %fusion.39 = (f32[48,128,4]{1,2,0:T(4,128)S(1)}, f32[48,128,4]{1,2,0:T(4,128)S(1)}, f32[48,128,4]{1,2,0:T(4,128)S(1)}, f32[48,128,4]{1,2,0:T(4,128)S(1)}) fusion(f32[4]{0:T(128)S(1)} %multiply_add_fusion.3, f32[48,128]{1,0:T(8,128)S(1)} %bitcast.167, f32[48,128]{1,0:T(8,128)S(1)} %bitcast.169), kind=kLoop, calls=%fused_computation.64 | loop fusion | flops 98304 | bytes 442384 | tf_op jit(solution)/shard_map/cos | solution.py:31
  4.9 0.1 mul.700
  5.0 0.9 copy_multiply_fusion
  5.8 0.2 add_bitcast_fusion
  6.1 0.5 fusion.30
  6.6 1.4 %fusion = f32[48,32,64]{2,1,0:T(8,128)S(1)} fusion(f32[48,128,32]{1,2,0:T(8,128)S(1)} %get-tuple-element.18, f32[48,128,32]{1,2,0:T(8,128)S(1)} %get-tuple-element.41, f32[48,128,32]{1,2,0:T(8,128)S(1)} %get-tuple-element.17, f32[48,128,32]{1,2,0:T(8,128)S(1)} %get-tuple-element.16, f32[48,128,32]{1,2,0:T(8,128)S(1)} %get-tuple-element.15), kind=kOutput, calls=%fused_computation.1 | convolution fusion | flops 153747456 | bytes 4325376 | tf_op jit(solution)/shard_map/ikx,iky->ixy/dot_general | solution.py:51
  8.0 0.5 copy.42
  8.5 1.1 convolution_bitcast_fusion.5
  9.6 1.7 %fusion.19 = bf16[48,2,32,32]{0,2,1,3:T(8,128)(2,1)S(1)} fusion(f32[48,32,2,32,1]{0,3,2,1,4:T(8,128)S(1)} %convolution_bitcast_fusion.5, f32[1,2,32,32]{2,3,1,0:T(8,128)S(1)} %get-tuple-element.36, f32[1,2,32,32]{2,3,1,0:T(8,128)S(1)} %get-tuple-element.35), kind=kOutput, calls=%fused_computation.24 | convolution fusion | flops 75698176 | bytes 606208 | tf_op jit(solution)/shard_map/ocpx,ixcq->iopq/dot_general | solution.py:55
  11.3 1.4 %copy.45 = bf16[48,2,32,32]{3,2,1,0:T(8,128)(2,1)S(1)} copy(bf16[48,2,32,32]{0,2,1,3:T(8,128)(2,1)S(1)} %fusion.19) | data formatting | bytes 393216 | tf_op jit(solution)/shard_map/convert_element_type | solution.py:56
  12.7 0.9 reshape.508
  13.7 0.1 copy.74
  13.9 28.0 %all_to_all.32 = bf16[4,12,2176]{2,0,1:T(4,128)(2,1)S(1)} all-to-all(bf16[4,12,2176]{2,0,1:T(4,128)(2,1)S(1)} %copy.47), channel_id=1, replica_groups=mesh['chan'=12,'tile'=64] {'chan'}, dimensions={1} | all-to-all | bytes 417792 | tf_op jit(solution)/shard_map/all_to_all | solution.py:141
  42.0 0.1 convert_reduce_fusion.2
  42.2 0.2 select_reduce_fusion
  42.4 0.3 convolution_convert_fusion
  42.7 1.0 all_to_all.25
  43.7 12.9 %all-to-all-start.1 = ((bf16[64,2,2176]{2,1,0:T(2,128)(2,1)}), bf16[64,2,2176]{2,1,0:T(2,128)(2,1)S(1)}, u32[]{:S(2)}, u32[]{:S(2)}) async-start(bf16[64,2,2176]{2,1,0:T(2,128)(2,1)} %all_to_all.25), calls=%async_computation.1 | async-start | bytes 1114112 | tf_op jit(solution)/shard_map/all_to_all | solution.py:148
  56.7 0.1 fusion.69
  56.9 0.1 fusion.70
  57.0 0.1 multiply_sine_fusion.1
  57.0 0.1 fusion.63
  57.2 17.4 %all-to-all-done.1 = bf16[64,2,2176]{2,1,0:T(2,128)(2,1)S(1)} async-done(((bf16[64,2,2176]{2,1,0:T(2,128)(2,1)}), bf16[64,2,2176]{2,1,0:T(2,128)(2,1)S(1)}, u32[]{:S(2)}, u32[]{:S(2)}) %all-to-all-start.1) | async-done | bytes 557088 | tf_op jit(solution)/shard_map/all_to_all | solution.py:148
  74.7 0.2 all_to_all.27
  74.9 0.2 convert_reduce_fusion
  75.1 0.3 copy.48
  75.4 3.0 %copy.49 = bf16[128,2,32,32]{3,2,1,0:T(8,128)(2,1)S(1)} copy(bf16[128,2,32,32]{0,3,2,1:T(8,128)(2,1)S(1)} %bitcast.164) | data formatting | bytes 1048576 | tf_op jit(solution)/shard_map/reshape | solution.py:149
  78.5 2.1 %fusion.11 = bf16[128,2,32,64]{3,2,1,0:T(8,128)(2,1)} fusion(bf16[128,2,32,32]{3,2,1,0:T(8,128)(2,1)S(1)} %copy.49, s32[128,32]{1,0:T(8,128)S(1)} %iota_add_fusion), kind=kOutput, calls=%fused_computation.12 | convolution fusion | flops 34340864 | bytes 1589248 | tf_op jit(solution)/shard_map/scpq,sqw->scpw/dot_general | solution.py:70
  80.5 3.2 %copy.72 = bf16[128,2,32,64]{0,3,1,2:T(8,128)(2,1)S(1)} copy(bf16[128,2,32,64]{3,2,1,0:T(8,128)(2,1)} %fusion.11) | data formatting | bytes 2097152 | tf_op jit(solution)/shard_map/reshape | solution.py:73
  83.8 0.4 convolution_bitcast_fusion.3
  84.2 0.6 convolution_bitcast_fusion.2
  84.8 0.2 multiply_subtract_fusion.2
  85.0 0.6 convolution_bitcast_fusion.1
  85.6 1.2 %copy.73 = f32[32,64,2,32]{3,2,1,0:T(2,128)S(1)} copy(f32[32,64,2,32]{1,0,3,2:T(8,128)S(1)} %convolution_bitcast_fusion.1) | data formatting | bytes 1048576 | tf_op jit(solution)/shard_map/reshape | solution.py:154
  86.9 2.0 %reshape.539 = f32[64,1,2048]{2,1,0:T(1,128)S(1)} reshape(f32[64,32,2,32]{3,2,1,0:T(2,128)S(1)} %bitcast.161) | data formatting | bytes 1048576
  88.9 23.4 %all_to_all.33 = f32[64,1,2048]{2,1,0:T(1,128)S(1)} all-to-all(f32[64,1,2048]{2,1,0:T(1,128)S(1)} %reshape.539), channel_id=1, replica_groups=mesh['chan'=12,'tile'=64] {'tile'}, dimensions={0} | all-to-all | bytes 1048576 | tf_op jit(solution)/shard_map/all_to_all | solution.py:155
  112.3 0.5 broadcast.726
  112.8 1.9 %reduce.8 = f32[64,2048]{1,0:T(8,128)S(1)} reduce(f32[64,1,2048]{2,1,0:T(1,128)S(1)} %all_to_all.33, f32[]{:T(128)} %broadcast.726), dimensions={1}, to_apply=%all_to_all.28.reduce_sub_computation | reduce | bytes 1048580 | tf_op jit(solution)/shard_map/all_to_all | solution.py:155
  114.7 1.8 %reshape.540 = f32[64,32,2,32]{3,2,1,0:T(2,128)S(1)} reshape(f32[64,2048]{1,0:T(8,128)S(1)} %reduce.8) | data formatting | bytes 1048576
  116.5 1.1 copy.54
  117.6 0.6 convolution_bitcast_fusion
  118.2 0.2 multiply_subtract_fusion.1
  118.4 0.4 fusion.21
  118.8 0.9 div.37
  (28 shorter events, 0.7 us)
Async XLA Ops:
  9.6 4.0 %copy-start = (s32[1,4,2]{1,2,0:T(2,128)S(1)}, s32[1,4,2]{1,2,0:T(2,128)}, u32[]{:S(2)}) copy-start(s32[1,4,2]{1,2,0:T(2,128)} %param.8) | copy-start | bytes 100
  9.6 4.0 %copy-start.1 = (s32[1,4,1]{1,2,0:T(1,128)S(1)}, s32[1,4,1]{1,2,0:T(1,128)}, u32[]{:S(2)}) copy-start(s32[1,4,1]{1,2,0:T(1,128)} %param.7) | copy-start | bytes 52
  43.7 30.9 %all-to-all-start.1 = ((bf16[64,2,2176]{2,1,0:T(2,128)(2,1)}), bf16[64,2,2176]{2,1,0:T(2,128)(2,1)S(1)}, u32[]{:S(2)}, u32[]{:S(2)}) async-start(bf16[64,2,2176]{2,1,0:T(2,128)(2,1)} %all_to_all.25), calls=%async_computation.1 | async-start | bytes 1114112 | tf_op jit(solution)/shard_map/all_to_all | solution.py:148
where the time goes:
time: 120 us
  blocking collectives  51.4 us (43%)
  local copies, waits for them, and re-layouts  19.3 us (16%)
  waiting for transfers between devices  17.4 us (14%)
  starting transfers between devices  12.9 us (11%)
  matrix products  9.27 us (8%)
  other arithmetic  8.34 us (7%)
    all_to_all x1, blocking collectives, per_device(): lax.all_to_all(payload, 'chan', split_axis=1, concat_axis=0, tiled=True)  28 us
    all_to_all x1, blocking collectives, per_device(): lax.all_to_all(half, 'tile', split_axis=0, concat_axis=0, tiled=True)  23.4 us
    all_to_all x1, waiting for transfers between devices, per_device(): lax.all_to_all(outgoing, 'tile', split_axis=0, concat_axis=0, tiled=True)  17.4 us
    all_to_all x1, starting transfers between devices, per_device(): lax.all_to_all(outgoing, 'tile', split_axis=0, concat_axis=0, tiled=True)  12.9 us
    unnamed x7, local copies, waits for them, and re-layouts  3.91 us
    reshape x1, local copies, waits for them, and re-layouts, place_windows(): shifted = shifted.reshape(slots, 2, NS, 2, NS)  3.2 us
    reshape x1, local copies, waits for them, and re-layouts, per_device(): windows = incoming[:, :cell_count].reshape(slot_count, 2, NS, NS)  2.98 us
  transfers between devices with their start and end apart: 1, of which 1 were waited for; matrix products, arithmetic and copies ran while one was open for 0% of the time, Pallas kernels for 0%

commit v1 on v0

--- a/solution.py
+++ b/solution.py
@@ -126,21 +126,19 @@
     band_rows = G // tile_count
     live_mask = (jnp.arange(blocks) < block_count.reshape(())).astype(jnp.float32)
     masked = samples[0] * live_mask[:, None, None, None]
-    item_count = blocks * channels
-    formed = form_subgrids(
-        masked.reshape(item_count, 2, steps_time), uv_coords[0].reshape(item_count, 2, steps_time)
-    )
-    cell_count = 2 * NS * NS
-    formed = formed.reshape(blocks, channels, cell_count)
     owners = block_owner[0, :, 0]
     cols = placement_map[0, :, 1]
-    meta = jnp.stack([owners, cols // NS, cols % NS], axis=1).astype(jnp.bfloat16)
-    meta = jnp.pad(meta, ((0, 0), (0, META - 3)))
-    meta = jnp.broadcast_to(meta[:, None, :], (blocks, channels, META))
-    payload = jnp.concatenate([formed, meta], axis=2)
+    meta = jnp.stack([owners, cols // NS, cols % NS], axis=1).astype(jnp.float32)
+    meta = jnp.pad(meta, ((0, 0), (0, steps_time - 3)))
+    meta = jnp.broadcast_to(meta[:, None, None, :], (blocks, channels, 1, steps_time))
+    payload = jnp.concatenate([masked, uv_coords[0], meta], axis=2)
     arrived = lax.all_to_all(payload, "chan", split_axis=1, concat_axis=0, tiled=True)
-    arrived = arrived.reshape(group_blocks, cell_count + META)
-    group_owners = arrived[:, cell_count].astype(jnp.int32)
+    arrived = arrived.reshape(group_blocks, 5, steps_time)
+    formed = form_subgrids(arrived[:, 0:2], arrived[:, 2:4])
+    cell_count = 2 * NS * NS
+    group_meta = arrived[:, 4, 0:META].astype(jnp.bfloat16)
+    arrived = jnp.concatenate([formed.reshape(group_blocks, cell_count), group_meta], axis=1)
+    group_owners = group_meta[:, 0].astype(jnp.int32)
     target = slot_targets(group_owners, tile_count, capacity)
     slot_count = tile_count * capacity
     pick = (jnp.arange(slot_count)[:, None] == target[None, :]).astype(jnp.bfloat16)

time: 120 us -> 119 us (level)
  blocking collectives: 51.4 us -> 23.4 us
  starting transfers between devices: 12.9 us -> 28.4 us
  waiting for transfers between devices: 17.4 us -> 27.6 us
  other arithmetic: 8.34 us -> 10.3 us
    all_to_all x1 -> x0, blocking collectives: 28 us -> none  [per_device(): lax.all_to_all(payload, 'chan', split_axis=1, concat_axis=0, tiled=True)]
    all_to_all x0 -> x1, starting transfers between devices: none -> 15.7 us  [per_device(): lax.all_to_all(payload, 'chan', split_axis=1, concat_axis=0, tiled=True)]
    all_to_all x0 -> x1, waiting for transfers between devices: none -> 10.2 us  [per_device(): lax.all_to_all(payload, 'chan', split_axis=1, concat_axis=0, tiled=True)]
    unnamed x7 -> x4, local copies, waits for them, and re-layouts: 3.91 us -> 4.7 us
  transfers between devices with their start and end apart: 1 -> 2, of which waited for: 1 -> 2; matrix products, arithmetic and copies ran while one was open for 0% -> 1% of each run, Pallas kernels for 0% -> 0%
where the time goes in v1:
time: 119 us
  starting transfers between devices  28.4 us (24%)
  waiting for transfers between devices  27.6 us (23%)
  blocking collectives  23.4 us (20%)
  local copies, waits for them, and re-layouts  18.9 us (16%)
  other arithmetic  10.3 us (9%)
  matrix products  9.28 us (8%)
    all_to_all x1, blocking collectives, per_device(): lax.all_to_all(half, 'tile', split_axis=0, concat_axis=0, tiled=True)  23.4 us
    all_to_all x1, waiting for transfers between devices, per_device(): lax.all_to_all(outgoing, 'tile', split_axis=0, concat_axis=0, tiled=True)  17.4 us
    all_to_all x1, starting transfers between devices, per_device(): lax.all_to_all(payload, 'chan', split_axis=1, concat_axis=0, tiled=True)  15.7 us
    all_to_all x1, starting transfers between devices, per_device(): lax.all_to_all(outgoing, 'tile', split_axis=0, concat_axis=0, tiled=True)  12.7 us
    all_to_all x1, waiting for transfers between devices, per_device(): lax.all_to_all(payload, 'chan', split_axis=1, concat_axis=0, tiled=True)  10.2 us
    unnamed x4, local copies, waits for them, and re-layouts  4.7 us
    reshape x1, local copies, waits for them, and re-layouts, place_windows(): shifted = shifted.reshape(slots, 2, NS, 2, NS)  3.2 us
    reshape x1, local copies, waits for them, and re-layouts, per_device(): windows = incoming[:, :cell_count].reshape(slot_count, 2, NS, NS)  2.98 us
  transfers between devices with their start and end apart: 2, of which 2 were waited for; matrix products, arithmetic and copies ran while one was open for 1% of the time, Pallas kernels for 0%

profile of v1, /device:TPU:1, one launch (start us, length us, event | category | flops | bytes accessed | tf_op | source)
XLA Modules:
  0.0 118.9 jit_solution(13657465356027299024)
XLA Ops:
  0.0 0.7 and_select_fusion.1
  0.7 0.7 add_convert_fusion
  1.4 0.1 copy.80
  2.1 0.8 copy.89
  3.0 0.9 bitcast_multiply_fusion.4
  3.8 0.7 pad_maximum_fusion.1
  4.5 15.7 %all-to-all-start = ((f32[4,12,5,128]{3,0,2,1:T(4,128)}), f32[4,12,5,128]{3,0,2,1:T(4,128)S(1)}, u32[]{:S(2)}, u32[]{:S(2)}) async-start(f32[4,12,5,128]{3,0,2,1:T(4,128)} %pad_maximum_fusion.1), calls=%async_computation | async-start | bytes 245760 | tf_op jit(solution)/shard_map/all_to_all | solution.py:135
  20.3 0.1 multiply_sine_fusion
  20.4 10.2 %all-to-all-done = f32[4,12,5,128]{3,0,2,1:T(4,128)S(1)} async-done(((f32[4,12,5,128]{3,0,2,1:T(4,128)}), f32[4,12,5,128]{3,0,2,1:T(4,128)S(1)}, u32[]{:S(2)}, u32[]{:S(2)}) %all-to-all-start) | async-done | bytes 122912 | tf_op jit(solution)/shard_map/all_to_all | solution.py:135
  30.7 1.5 %fusion.38 = (f32[48,128,8]{1,2,0:T(8,128)S(1)}, f32[48,128,8]{1,2,0:T(8,128)S(1)}, f32[48,128,8]{1,2,0:T(8,128)S(1)}, f32[48,128,8]{1,2,0:T(8,128)S(1)}) fusion(f32[8]{0:T(128)S(1)} %iota_convert_fusion, f32[48,128]{1,0:T(8,128)S(1)} %get-tuple-element.22, f32[48,128]{1,0:T(8,128)S(1)} %get-tuple-element.20), kind=kLoop, calls=%fused_computation.59 | loop fusion | flops 196608 | bytes 835616 | tf_op jit(solution)/shard_map/cos | solution.py:32
  32.1 1.6 %fusion.42 = (f32[48,128,4]{1,2,0:T(4,128)S(1)}, f32[48,128,4]{1,2,0:T(4,128)S(1)}, f32[48,128,4]{1,2,0:T(4,128)S(1)}, f32[48,128,4]{1,2,0:T(4,128)S(1)}) fusion(f32[4]{0:T(128)S(1)} %multiply_add_fusion.3, f32[48,128]{1,0:T(8,128)S(1)} %get-tuple-element.22, f32[48,128]{1,0:T(8,128)S(1)} %get-tuple-element.20), kind=kLoop, calls=%fused_computation.67 | loop fusion | flops 98304 | bytes 442384 | tf_op jit(solution)/shard_map/cos | solution.py:31
  33.7 0.2 add_bitcast_fusion
  34.0 0.5 fusion.30
  34.4 1.4 %fusion = f32[48,32,64]{2,1,0:T(8,128)S(1)} fusion(f32[48,128,32]{1,2,0:T(8,128)S(1)} %get-tuple-element.18, f32[48,128,32]{1,2,0:T(8,128)S(1)} %get-tuple-element.41, f32[48,128,32]{1,2,0:T(8,128)S(1)} %get-tuple-element.17, f32[48,128,32]{1,2,0:T(8,128)S(1)} %get-tuple-element.16, f32[48,128,32]{1,2,0:T(8,128)S(1)} %get-tuple-element.15), kind=kOutput, calls=%fused_computation.1 | convolution fusion | flops 153747456 | bytes 4325376 | tf_op jit(solution)/shard_map/ikx,iky->ixy/dot_general | solution.py:51
  35.9 0.5 copy.50
  36.4 1.1 convolution_bitcast_fusion.5
  37.4 1.7 %fusion.19 = bf16[48,2,32,32]{0,2,1,3:T(8,128)(2,1)S(1)} fusion(f32[48,32,2,32,1]{0,3,2,1,4:T(8,128)S(1)} %convolution_bitcast_fusion.5, f32[1,2,32,32]{2,3,1,0:T(8,128)S(1)} %get-tuple-element.36, f32[1,2,32,32]{2,3,1,0:T(8,128)S(1)} %get-tuple-element.35), kind=kOutput, calls=%fused_computation.24 | convolution fusion | flops 75698176 | bytes 606208 | tf_op jit(solution)/shard_map/ocpx,ixcq->iopq/dot_general | solution.py:55
  39.2 1.4 %copy.53 = bf16[48,2,32,32]{3,2,1,0:T(8,128)(2,1)S(1)} copy(bf16[48,2,32,32]{0,2,1,3:T(8,128)(2,1)S(1)} %fusion.19) | data formatting | bytes 393216 | tf_op jit(solution)/shard_map/convert_element_type | solution.py:56
  40.6 0.8 reshape.509
  41.4 0.1 convert_reduce_fusion.2
  41.7 0.2 select_reduce_fusion
  41.9 0.3 convolution_convert_fusion
  42.2 1.0 all_to_all.25
  43.2 12.7 %all-to-all-start.1 = ((bf16[64,2,2176]{2,1,0:T(2,128)(2,1)}), bf16[64,2,2176]{2,1,0:T(2,128)(2,1)S(1)}, u32[]{:S(2)}, u32[]{:S(2)}) async-start(bf16[64,2,2176]{2,1,0:T(2,128)(2,1)} %all_to_all.25), calls=%async_computation.1 | async-start | bytes 1114112 | tf_op jit(solution)/shard_map/all_to_all | solution.py:146
  55.9 0.1 fusion.72
  56.3 0.1 fusion.66
  56.4 17.4 %all-to-all-done.1 = bf16[64,2,2176]{2,1,0:T(2,128)(2,1)S(1)} async-done(((bf16[64,2,2176]{2,1,0:T(2,128)(2,1)}), bf16[64,2,2176]{2,1,0:T(2,128)(2,1)S(1)}, u32[]{:S(2)}, u32[]{:S(2)}) %all-to-all-start.1) | async-done | bytes 557088 | tf_op jit(solution)/shard_map/all_to_all | solution.py:146
  73.9 0.2 all_to_all.27
  74.2 0.2 convert_reduce_fusion
  74.3 0.3 copy.54
  74.6 3.0 %copy.55 = bf16[128,2,32,32]{3,2,1,0:T(8,128)(2,1)S(1)} copy(bf16[128,2,32,32]{0,3,2,1:T(8,128)(2,1)S(1)} %bitcast.166) | data formatting | bytes 1048576 | tf_op jit(solution)/shard_map/reshape | solution.py:147
  77.7 2.1 %fusion.11 = bf16[128,2,32,64]{3,2,1,0:T(8,128)(2,1)} fusion(bf16[128,2,32,32]{3,2,1,0:T(8,128)(2,1)S(1)} %copy.55, s32[128,32]{1,0:T(8,128)S(1)} %iota_add_fusion), kind=kOutput, calls=%fused_computation.12 | convolution fusion | flops 34340864 | bytes 1589248 | tf_op jit(solution)/shard_map/scpq,sqw->scpw/dot_general | solution.py:70
  79.8 3.2 %copy.78 = bf16[128,2,32,64]{0,3,1,2:T(8,128)(2,1)S(1)} copy(bf16[128,2,32,64]{3,2,1,0:T(8,128)(2,1)} %fusion.11) | data formatting | bytes 2097152 | tf_op jit(solution)/shard_map/reshape | solution.py:73
  83.0 0.4 convolution_bitcast_fusion.3
  83.4 0.6 convolution_bitcast_fusion.2
  84.0 0.2 multiply_subtract_fusion.2
  84.2 0.6 convolution_bitcast_fusion.1
  84.8 1.2 %copy.79 = f32[32,64,2,32]{3,2,1,0:T(2,128)S(1)} copy(f32[32,64,2,32]{1,0,3,2:T(8,128)S(1)} %convolution_bitcast_fusion.1) | data formatting | bytes 1048576 | tf_op jit(solution)/shard_map/reshape | solution.py:152
  86.1 2.0 %reshape.539 = f32[64,1,2048]{2,1,0:T(1,128)S(1)} reshape(f32[64,32,2,32]{3,2,1,0:T(2,128)S(1)} %bitcast.163) | data formatting | bytes 1048576
  88.1 23.4 %all_to_all.32 = f32[64,1,2048]{2,1,0:T(1,128)S(1)} all-to-all(f32[64,1,2048]{2,1,0:T(1,128)S(1)} %reshape.539), channel_id=1, replica_groups=mesh['chan'=12,'tile'=64] {'tile'}, dimensions={0} | all-to-all | bytes 1048576 | tf_op jit(solution)/shard_map/all_to_all | solution.py:153
  111.5 0.5 broadcast.725
  112.0 1.9 %reduce.8 = f32[64,2048]{1,0:T(8,128)S(1)} reduce(f32[64,1,2048]{2,1,0:T(1,128)S(1)} %all_to_all.32, f32[]{:T(128)} %broadcast.725), dimensions={1}, to_apply=%all_to_all.28.reduce_sub_computation | reduce | bytes 1048580 | tf_op jit(solution)/shard_map/all_to_all | solution.py:153
  113.9 1.8 %reshape.540 = f32[64,32,2,32]{3,2,1,0:T(2,128)S(1)} reshape(f32[64,2048]{1,0:T(8,128)S(1)} %reduce.8) | data formatting | bytes 1048576
  115.7 1.1 copy.60
  116.8 0.6 convolution_bitcast_fusion
  117.4 0.2 multiply_subtract_fusion.1
  117.6 0.4 fusion.21
  118.0 0.9 div.37
  (22 shorter events, 0.7 us)
Async XLA Ops:
  4.5 26.1 %all-to-all-start = ((f32[4,12,5,128]{3,0,2,1:T(4,128)}), f32[4,12,5,128]{3,0,2,1:T(4,128)S(1)}, u32[]{:S(2)}, u32[]{:S(2)}) async-start(f32[4,12,5,128]{3,0,2,1:T(4,128)} %pad_maximum_fusion.1), calls=%async_computation | async-start | bytes 245760 | tf_op jit(solution)/shard_map/all_to_all | solution.py:135
  43.2 30.7 %all-to-all-start.1 = ((bf16[64,2,2176]{2,1,0:T(2,128)(2,1)}), bf16[64,2,2176]{2,1,0:T(2,128)(2,1)S(1)}, u32[]{:S(2)}, u32[]{:S(2)}) async-start(bf16[64,2,2176]{2,1,0:T(2,128)(2,1)} %all_to_all.25), calls=%async_computation.1 | async-start | bytes 1114112 | tf_op jit(solution)/shard_map/all_to_all | solution.py:146

commit v2 on v1

--- a/solution.py
+++ b/solution.py
@@ -149,9 +149,9 @@
     col_lo = incoming[:, cell_count + 2].astype(jnp.int32)
     tile_grid = place_windows(windows, col_hi, col_lo, G // NS)
     half = transform_rows(tile_grid)
-    half = half.reshape(tile_count, G // tile_count, 2, band_rows)
+    half = half.reshape(tile_count, G // tile_count, 2, band_rows).astype(jnp.bfloat16)
     turned = lax.all_to_all(half, "tile", split_axis=0, concat_axis=0, tiled=True)
-    dirty_image = transform_cols(turned) / G
+    dirty_image = transform_cols(turned.astype(jnp.float32)) / G
     return dirty_image[None]
 
 

time: 119 us -> 109 us (0.916)
  blocking collectives: 23.4 us -> 18 us
  local copies, waits for them, and re-layouts: 18.9 us -> 15.9 us
  other arithmetic: 10.3 us -> 8.45 us
    all_to_all x1, blocking collectives: 23.4 us -> 18 us  [per_device(): lax.all_to_all(half, 'tile', split_axis=0, concat_axis=0, tiled=True)]
    unnamed x4, local copies, waits for them, and re-layouts: 4.7 us -> 2.4 us
    all_to_all x1 -> x0, other arithmetic: 1.88 us -> none  [per_device(): lax.all_to_all(half, 'tile', split_axis=0, concat_axis=0, tiled=True)]
    reshape x1 -> x0, local copies, waits for them, and re-layouts: 1.24 us -> none  [per_device(): half = half.reshape(tile_count, G // tile_count, 2, band_rows)]
where the time goes in v2:
time: 109 us; the launch traced here: 108 us
  starting transfers between devices  28.4 us (26%)
  waiting for transfers between devices  27.6 us (25%)
  blocking collectives  18 us (17%)
  local copies, waits for them, and re-layouts  15.9 us (15%)
  matrix products  9.12 us (8%)
  other arithmetic  8.45 us (8%)
    all_to_all x1, blocking collectives, per_device(): lax.all_to_all(half, 'tile', split_axis=0, concat_axis=0, tiled=True)  18 us
    all_to_all x1, waiting for transfers between devices, per_device(): lax.all_to_all(outgoing, 'tile', split_axis=0, concat_axis=0, tiled=True)  17.4 us
    all_to_all x1, starting transfers between devices, per_device(): lax.all_to_all(payload, 'chan', split_axis=1, concat_axis=0, tiled=True)  15.7 us
    all_to_all x1, starting transfers between devices, per_device(): lax.all_to_all(outgoing, 'tile', split_axis=0, concat_axis=0, tiled=True)  12.7 us
    all_to_all x1, waiting for transfers between devices, per_device(): lax.all_to_all(payload, 'chan', split_axis=1, concat_axis=0, tiled=True)  10.2 us
    reshape x1, local copies, waits for them, and re-layouts, place_windows(): shifted = shifted.reshape(slots, 2, NS, 2, NS)  3.2 us
    reshape x1, local copies, waits for them, and re-layouts, per_device(): windows = incoming[:, :cell_count].reshape(slot_count, 2, NS, NS)  2.98 us
    unnamed x4, local copies, waits for them, and re-layouts  2.4 us
  transfers between devices with their start and end apart: 2, of which 2 were waited for; matrix products, arithmetic and copies ran while one was open for 1% of the time, Pallas kernels for 0%

profile of v2, /device:TPU:1, one launch (start us, length us, event | category | flops | bytes accessed | tf_op | source)
XLA Modules:
  0.0 108.5 jit_solution(18005556423951056678)
XLA Ops:
  0.0 0.7 and_select_fusion.1
  0.7 0.7 add_convert_fusion
  1.4 0.1 copy.80
  2.1 0.8 copy.89
  3.0 0.9 bitcast_multiply_fusion.4
  3.8 0.7 pad_maximum_fusion.1
  4.5 15.7 %all-to-all-start = ((f32[4,12,5,128]{3,0,2,1:T(4,128)}), f32[4,12,5,128]{3,0,2,1:T(4,128)S(1)}, u32[]{:S(2)}, u32[]{:S(2)}) async-start(f32[4,12,5,128]{3,0,2,1:T(4,128)} %pad_maximum_fusion.1), calls=%async_computation | async-start | bytes 245760 | tf_op jit(solution)/shard_map/all_to_all | solution.py:135
  20.3 0.1 multiply_sine_fusion
  20.4 10.2 %all-to-all-done = f32[4,12,5,128]{3,0,2,1:T(4,128)S(1)} async-done(((f32[4,12,5,128]{3,0,2,1:T(4,128)}), f32[4,12,5,128]{3,0,2,1:T(4,128)S(1)}, u32[]{:S(2)}, u32[]{:S(2)}) %all-to-all-start) | async-done | bytes 122912 | tf_op jit(solution)/shard_map/all_to_all | solution.py:135
  30.7 1.5 %fusion.40 = (f32[48,128,8]{1,2,0:T(8,128)S(1)}, f32[48,128,8]{1,2,0:T(8,128)S(1)}, f32[48,128,8]{1,2,0:T(8,128)S(1)}, f32[48,128,8]{1,2,0:T(8,128)S(1)}) fusion(f32[8]{0:T(128)S(1)} %iota_convert_fusion, f32[48,128]{1,0:T(8,128)S(1)} %get-tuple-element.22, f32[48,128]{1,0:T(8,128)S(1)} %get-tuple-element.20), kind=kLoop, calls=%fused_computation.61 | loop fusion | flops 196608 | bytes 835616 | tf_op jit(solution)/shard_map/cos | solution.py:32
  32.1 1.6 %fusion.44 = (f32[48,128,4]{1,2,0:T(4,128)S(1)}, f32[48,128,4]{1,2,0:T(4,128)S(1)}, f32[48,128,4]{1,2,0:T(4,128)S(1)}, f32[48,128,4]{1,2,0:T(4,128)S(1)}) fusion(f32[4]{0:T(128)S(1)} %multiply_add_fusion.3, f32[48,128]{1,0:T(8,128)S(1)} %get-tuple-element.22, f32[48,128]{1,0:T(8,128)S(1)} %get-tuple-element.20), kind=kLoop, calls=%fused_computation.69 | loop fusion | flops 98304 | bytes 442384 | tf_op jit(solution)/shard_map/cos | solution.py:31
  33.7 0.2 add_bitcast_fusion
  34.0 0.5 fusion.31
  34.4 1.4 %fusion = f32[48,32,64]{2,1,0:T(8,128)S(1)} fusion(f32[48,128,32]{1,2,0:T(8,128)S(1)} %get-tuple-element.18, f32[48,128,32]{1,2,0:T(8,128)S(1)} %get-tuple-element.41, f32[48,128,32]{1,2,0:T(8,128)S(1)} %get-tuple-element.17, f32[48,128,32]{1,2,0:T(8,128)S(1)} %get-tuple-element.16, f32[48,128,32]{1,2,0:T(8,128)S(1)} %get-tuple-element.15), kind=kOutput, calls=%fused_computation.1 | convolution fusion | flops 153747456 | bytes 4325376 | tf_op jit(solution)/shard_map/ikx,iky->ixy/dot_general | solution.py:51
  35.9 0.5 copy.50
  36.4 1.1 convolution_bitcast_fusion.5
  37.4 1.7 %fusion.20 = bf16[48,2,32,32]{0,2,1,3:T(8,128)(2,1)S(1)} fusion(f32[48,32,2,32,1]{0,3,2,1,4:T(8,128)S(1)} %convolution_bitcast_fusion.5, f32[1,2,32,32]{2,3,1,0:T(8,128)S(1)} %get-tuple-element.36, f32[1,2,32,32]{2,3,1,0:T(8,128)S(1)} %get-tuple-element.35), kind=kOutput, calls=%fused_computation.25 | convolution fusion | flops 75698176 | bytes 606208 | tf_op jit(solution)/shard_map/ocpx,ixcq->iopq/dot_general | solution.py:55
  39.2 1.4 %copy.53 = bf16[48,2,32,32]{3,2,1,0:T(8,128)(2,1)S(1)} copy(bf16[48,2,32,32]{0,2,1,3:T(8,128)(2,1)S(1)} %fusion.20) | data formatting | bytes 393216 | tf_op jit(solution)/shard_map/convert_element_type | solution.py:56
  40.6 0.8 reshape.508
  41.4 0.1 convert_reduce_fusion.2
  41.7 0.2 select_reduce_fusion
  41.9 0.3 convolution_convert_fusion
  42.2 1.0 all_to_all.25
  43.2 12.7 %all-to-all-start.1 = ((bf16[64,2,2176]{2,1,0:T(2,128)(2,1)}), bf16[64,2,2176]{2,1,0:T(2,128)(2,1)S(1)}, u32[]{:S(2)}, u32[]{:S(2)}) async-start(bf16[64,2,2176]{2,1,0:T(2,128)(2,1)} %all_to_all.25), calls=%async_computation.1 | async-start | bytes 1114112 | tf_op jit(solution)/shard_map/all_to_all | solution.py:146
  55.9 0.1 fusion.74
  56.1 0.1 fusion.76
  56.2 0.1 multiply_sine_fusion.1
  56.3 0.1 fusion.68
  56.4 17.4 %all-to-all-done.1 = bf16[64,2,2176]{2,1,0:T(2,128)(2,1)S(1)} async-done(((bf16[64,2,2176]{2,1,0:T(2,128)(2,1)}), bf16[64,2,2176]{2,1,0:T(2,128)(2,1)S(1)}, u32[]{:S(2)}, u32[]{:S(2)}) %all-to-all-start.1) | async-done | bytes 557088 | tf_op jit(solution)/shard_map/all_to_all | solution.py:146
  73.9 0.2 all_to_all.27
  74.2 0.2 convert_reduce_fusion
  74.3 0.3 copy.54
  74.6 3.0 %copy.55 = bf16[128,2,32,32]{3,2,1,0:T(8,128)(2,1)S(1)} copy(bf16[128,2,32,32]{0,3,2,1:T(8,128)(2,1)S(1)} %bitcast.170) | data formatting | bytes 1048576 | tf_op jit(solution)/shard_map/reshape | solution.py:147
  77.7 2.0 %fusion.11 = bf16[128,2,32,64]{3,2,1,0:T(8,128)(2,1)} fusion(bf16[128,2,32,32]{3,2,1,0:T(8,128)(2,1)S(1)} %copy.55, s32[128,32]{1,0:T(8,128)S(1)} %iota_add_fusion), kind=kOutput, calls=%fused_computation.12 | convolution fusion | flops 34340864 | bytes 1589248 | tf_op jit(solution)/shard_map/scpq,sqw->scpw/dot_general | solution.py:70
  79.7 3.2 %copy.78 = bf16[128,2,32,64]{0,3,1,2:T(8,128)(2,1)S(1)} copy(bf16[128,2,32,64]{3,2,1,0:T(8,128)(2,1)} %fusion.11) | data formatting | bytes 2097152 | tf_op jit(solution)/shard_map/reshape | solution.py:73
  83.0 0.4 convolution_bitcast_fusion.3
  83.4 0.6 convolution_bitcast_fusion.2
  84.0 0.2 multiply_subtract_fusion.2
  84.2 0.6 fusion.21
  84.8 0.9 copy.79
  85.7 1.0 reshape.537
  86.7 18.0 %all_to_all.32 = bf16[64,2,1024]{2,1,0:T(2,128)(2,1)S(1)} all-to-all(bf16[64,2,1024]{2,1,0:T(2,128)(2,1)S(1)} %reshape.537), channel_id=1, replica_groups=mesh['chan'=12,'tile'=64] {'tile'}, dimensions={0} | all-to-all | bytes 524288 | tf_op jit(solution)/shard_map/all_to_all | solution.py:153
  104.8 0.5 reshape.538
  105.3 1.2 %copy.60 = bf16[64,32,2,32]{0,3,2,1:T(8,128)(2,1)S(1)} copy(bf16[64,32,2,32]{3,2,1,0:T(2,128)(2,1)S(1)} %reshape.538) | data formatting | bytes 524288 | tf_op jit(solution)/shard_map/all_to_all | solution.py:153
  106.5 0.5 convolution_bitcast_fusion
  107.0 0.2 multiply_subtract_fusion.1
  107.2 0.4 fusion.23
  107.6 0.9 div.37
  (20 shorter events, 0.5 us)
Async XLA Ops:
  4.5 26.1 %all-to-all-start = ((f32[4,12,5,128]{3,0,2,1:T(4,128)}), f32[4,12,5,128]{3,0,2,1:T(4,128)S(1)}, u32[]{:S(2)}, u32[]{:S(2)}) async-start(f32[4,12,5,128]{3,0,2,1:T(4,128)} %pad_maximum_fusion.1), calls=%async_computation | async-start | bytes 245760 | tf_op jit(solution)/shard_map/all_to_all | solution.py:135
  43.2 30.7 %all-to-all-start.1 = ((bf16[64,2,2176]{2,1,0:T(2,128)(2,1)}), bf16[64,2,2176]{2,1,0:T(2,128)(2,1)S(1)}, u32[]{:S(2)}, u32[]{:S(2)}) async-start(bf16[64,2,2176]{2,1,0:T(2,128)(2,1)} %all_to_all.25), calls=%async_computation.1 | async-start | bytes 1114112 | tf_op jit(solution)/shard_map/all_to_all | solution.py:146

commit v3 on v2

--- a/solution.py
+++ b/solution.py
@@ -44,16 +44,25 @@
     vis_imag = masked[:, 1, :, None]
     weight_real = vis_real * cos_u - vis_imag * sin_u
     weight_imag = vis_real * sin_u + vis_imag * cos_u
-    left = jnp.concatenate([weight_real, weight_imag], axis=1)
+    table_real, table_imag = phase_table(NS, NS, NS, -1.0)
+    table = jnp.stack(
+        [
+            jnp.concatenate([table_real, table_imag], axis=1),
+            jnp.concatenate([-table_imag, table_real], axis=1),
+        ]
+    )
+    row_side = jnp.einsum(
+        "ikcx,cxn->ikn", jnp.stack([weight_real, weight_imag], axis=2), table, precision=HIGH
+    )
+    col_side = jnp.einsum(
+        "ikcx,cxn->ikn", jnp.stack([cos_v, sin_v], axis=2), table, precision=HIGH
+    )
+    left = jnp.concatenate([row_side[:, :, :NS], row_side[:, :, NS:]], axis=1)
     right = jnp.concatenate(
-        [jnp.concatenate([cos_v, sin_v], axis=2), jnp.concatenate([-sin_v, cos_v], axis=2)], axis=1
+        [col_side, jnp.concatenate([-col_side[:, :, NS:], col_side[:, :, :NS]], axis=2)], axis=1
     )
-    image = jnp.einsum("ikx,iky->ixy", left, right, precision=HIGH)
-    image = image.reshape(count, NS, 2, NS)
-    table = block_matrix(*phase_table(NS, NS, NS, -1.0))
-    half = jnp.einsum("ixcy,ocyq->ixoq", image, table, precision=HIGHEST)
-    full = jnp.einsum("ocpx,ixcq->iopq", table, half, precision=HIGHEST)
-    return (full / (NS * NS)).astype(jnp.bfloat16)
+    full = jnp.einsum("ikp,ikn->ipn", left, right, precision=HIGH)
+    return (full.reshape(count, NS, 2, NS) / (NS * NS)).astype(jnp.bfloat16)
 
 
 def slot_targets(owners, tile_count, capacity):
@@ -144,7 +153,7 @@
     pick = (jnp.arange(slot_count)[:, None] == target[None, :]).astype(jnp.bfloat16)
     outgoing = jnp.dot(pick, arrived, preferred_element_type=jnp.float32).astype(jnp.bfloat16)
     incoming = lax.all_to_all(outgoing, "tile", split_axis=0, concat_axis=0, tiled=True)
-    windows = incoming[:, :cell_count].reshape(slot_count, 2, NS, NS)
+    windows = incoming[:, :cell_count].reshape(slot_count, NS, 2, NS).transpose(0, 2, 1, 3)
     col_hi = incoming[:, cell_count + 1].astype(jnp.int32)
     col_lo = incoming[:, cell_count + 2].astype(jnp.int32)
     tile_grid = place_windows(windows, col_hi, col_lo, G // NS)

time: 109 us -> 106 us (0.972)
  local copies, waits for them, and re-layouts: 15.9 us -> 13.7 us
    reshape x2 -> x1, local copies, waits for them, and re-layouts: 3.81 us -> 2.98 us  [per_device(): incoming[:, :cell_count].reshape(slot_count, NS, 2, NS)]
where the time goes in v3:
time: 106 us; the launch traced here: 105 us
  starting transfers between devices  28.4 us (27%)
  waiting for transfers between devices  27.6 us (26%)
  blocking collectives  18.1 us (17%)
  local copies, waits for them, and re-layouts  13.7 us (13%)
  other arithmetic  8.54 us (8%)
  matrix products  8.07 us (8%)
    all_to_all x1, blocking collectives, per_device(): lax.all_to_all(half, 'tile', split_axis=0, concat_axis=0, tiled=True)  18.1 us
    all_to_all x1, waiting for transfers between devices, per_device(): lax.all_to_all(outgoing, 'tile', split_axis=0, concat_axis=0, tiled=True)  17.4 us
    all_to_all x1, starting transfers between devices, per_device(): lax.all_to_all(payload, 'chan', split_axis=1, concat_axis=0, tiled=True)  15.7 us
    all_to_all x1, starting transfers between devices, per_device(): lax.all_to_all(outgoing, 'tile', split_axis=0, concat_axis=0, tiled=True)  12.7 us
    all_to_all x1, waiting for transfers between devices, per_device(): lax.all_to_all(payload, 'chan', split_axis=1, concat_axis=0, tiled=True)  10.1 us
    reshape x1, local copies, waits for them, and re-layouts, place_windows(): shifted = shifted.reshape(slots, 2, NS, 2, NS)  3.2 us
    reshape x1, local copies, waits for them, and re-layouts, per_device(): incoming[:, :cell_count].reshape(slot_count, NS, 2, NS)  2.98 us
    unnamed x4, local copies, waits for them, and re-layouts  2.4 us
  transfers between devices with their start and end apart: 2, of which 2 were waited for; matrix products, arithmetic and copies ran while one was open for 1% of the time, Pallas kernels for 0%

profile of v3, /device:TPU:1, one launch (start us, length us, event | category | flops | bytes accessed | tf_op | source)
XLA Modules:
  0.0 105.3 jit_solution(18161114604341660111)
XLA Ops:
  0.0 0.7 and_select_fusion.1
  0.7 0.7 add_convert_fusion
  1.4 0.1 copy.59
  2.1 0.8 copy.66
  3.0 0.9 bitcast_multiply_fusion.4
  3.8 0.7 pad_maximum_fusion.1
  4.5 15.7 %all-to-all-start = ((f32[4,12,5,128]{3,0,2,1:T(4,128)}), f32[4,12,5,128]{3,0,2,1:T(4,128)S(1)}, u32[]{:S(2)}, u32[]{:S(2)}) async-start(f32[4,12,5,128]{3,0,2,1:T(4,128)} %pad_maximum_fusion.1), calls=%async_computation | async-start | bytes 245760 | tf_op jit(solution)/shard_map/all_to_all | solution.py:144
  20.3 0.1 fusion.100
  20.5 10.1 %all-to-all-done = f32[4,12,5,128]{3,0,2,1:T(4,128)S(1)} async-done(((f32[4,12,5,128]{3,0,2,1:T(4,128)}), f32[4,12,5,128]{3,0,2,1:T(4,128)S(1)}, u32[]{:S(2)}, u32[]{:S(2)}) %all-to-all-start) | async-done | bytes 122912 | tf_op jit(solution)/shard_map/all_to_all | solution.py:144
  30.7 1.5 %fusion.55 = (f32[48,128,8]{1,2,0:T(8,128)S(1)}, f32[48,128,8]{1,2,0:T(8,128)S(1)}, f32[48,128,8]{1,2,0:T(8,128)S(1)}, f32[48,128,8]{1,2,0:T(8,128)S(1)}) fusion(f32[8]{0:T(128)S(1)} %iota_convert_fusion, f32[48,128]{1,0:T(8,128)S(1)} %get-tuple-element.26, f32[48,128]{1,0:T(8,128)S(1)} %get-tuple-element.24), kind=kLoop, calls=%fused_computation.66 | loop fusion | flops 196608 | bytes 835616 | tf_op jit(solution)/shard_map/cos | solution.py:32
  32.1 1.6 %fusion.59 = (f32[48,128,4]{1,2,0:T(4,128)S(1)}, f32[48,128,4]{1,2,0:T(4,128)S(1)}, f32[48,128,4]{1,2,0:T(4,128)S(1)}, f32[48,128,4]{1,2,0:T(4,128)S(1)}) fusion(f32[4]{0:T(128)S(1)} %multiply_add_fusion.3, f32[48,128]{1,0:T(8,128)S(1)} %get-tuple-element.26, f32[48,128]{1,0:T(8,128)S(1)} %get-tuple-element.24), kind=kLoop, calls=%fused_computation.74 | loop fusion | flops 98304 | bytes 442384 | tf_op jit(solution)/shard_map/cos | solution.py:31
  33.7 0.3 fusion.42
  34.1 0.8 fusion.29
  34.9 0.1 fusion.114
  35.0 0.2 subtract_bitcast_fusion
  35.3 0.8 fusion.26
  36.1 0.2 slice_negate_fusion
  36.3 1.5 %multiply_convert_fusion = bf16[48,32,64]{2,1,0:T(8,128)(2,1)S(1)} fusion(f32[48,128,32]{1,2,0:T(8,128)S(1)} %get-tuple-element.14, f32[48,128,32]{1,2,0:T(8,128)S(1)} %get-tuple-element.13, f32[48,128,64]{1,2,0:T(8,128)S(1)} %fusion.26, f32[48,128,32]{1,2,0:T(8,128)S(1)} %get-tuple-element.12, f32[48,128,32]{1,2,0:T(8,128)S(1)} %get-tuple-element.11), kind=kOutput, calls=%fused_computation.48 | convolution fusion | flops 153157632 | bytes 4915200 | tf_op jit(solution)/shard_map/ikp,ikn->ipn/dot_general | solution.py:64
  37.8 0.4 convert_element_type.189
  38.2 0.1 convert_reduce_fusion.2
  38.4 0.2 select_reduce_fusion
  38.6 0.3 convolution_convert_fusion
  38.9 1.0 all_to_all.25
  39.9 12.7 %all-to-all-start.1 = ((bf16[64,2,2176]{2,1,0:T(2,128)(2,1)}), bf16[64,2,2176]{2,1,0:T(2,128)(2,1)S(1)}, u32[]{:S(2)}, u32[]{:S(2)}) async-start(bf16[64,2,2176]{2,1,0:T(2,128)(2,1)} %all_to_all.25), calls=%async_computation.1 | async-start | bytes 1114112 | tf_op jit(solution)/shard_map/all_to_all | solution.py:155
  52.7 0.1 fusion.96
  52.8 0.1 fusion.98
  52.9 0.1 fusion.102
  53.0 0.1 fusion.89
  53.2 17.4 %all-to-all-done.1 = bf16[64,2,2176]{2,1,0:T(2,128)(2,1)S(1)} async-done(((bf16[64,2,2176]{2,1,0:T(2,128)(2,1)}), bf16[64,2,2176]{2,1,0:T(2,128)(2,1)S(1)}, u32[]{:S(2)}, u32[]{:S(2)}) %all-to-all-start.1) | async-done | bytes 557088 | tf_op jit(solution)/shard_map/all_to_all | solution.py:155
  70.7 0.2 all_to_all.27
  70.9 0.2 convert_reduce_fusion
  71.1 0.3 copy.39
  71.4 3.0 %copy.40 = bf16[128,32,2,32]{3,1,2,0:T(8,128)(2,1)S(1)} copy(bf16[128,32,2,32]{0,3,2,1:T(8,128)(2,1)S(1)} %bitcast.152) | data formatting | bytes 1048576 | tf_op jit(solution)/shard_map/reshape | solution.py:156
  74.5 2.0 %fusion.10 = bf16[128,2,32,64]{3,2,1,0:T(8,128)(2,1)} fusion(bf16[128,32,2,32]{3,1,2,0:T(8,128)(2,1)S(1)} %copy.40, s32[128,32]{1,0:T(8,128)S(1)} %iota_add_fusion), kind=kOutput, calls=%fused_computation.11 | convolution fusion | flops 34340864 | bytes 1589248 | tf_op jit(solution)/shard_map/scpq,sqw->scpw/dot_general | solution.py:79
  76.5 3.2 %copy.57 = bf16[128,2,32,64]{0,3,1,2:T(8,128)(2,1)S(1)} copy(bf16[128,2,32,64]{3,2,1,0:T(8,128)(2,1)} %fusion.10) | data formatting | bytes 2097152 | tf_op jit(solution)/shard_map/reshape | solution.py:82
  79.7 0.4 convolution_bitcast_fusion.3
  80.1 0.6 convolution_bitcast_fusion.2
  80.8 0.2 multiply_subtract_fusion.2
  80.9 0.6 fusion.33
  81.6 0.9 copy.58
  82.5 1.0 reshape.703
  83.5 18.1 %all_to_all.32 = bf16[64,2,1024]{2,1,0:T(2,128)(2,1)S(1)} all-to-all(bf16[64,2,1024]{2,1,0:T(2,128)(2,1)S(1)} %reshape.703), channel_id=1, replica_groups=mesh['chan'=12,'tile'=64] {'tile'}, dimensions={0} | all-to-all | bytes 524288 | tf_op jit(solution)/shard_map/all_to_all | solution.py:162
  101.6 0.5 reshape.704
  102.1 1.2 %copy.45 = bf16[64,32,2,32]{0,3,2,1:T(8,128)(2,1)S(1)} copy(bf16[64,32,2,32]{3,2,1,0:T(2,128)(2,1)S(1)} %reshape.704) | data formatting | bytes 524288 | tf_op jit(solution)/shard_map/all_to_all | solution.py:162
  103.3 0.5 convolution_bitcast_fusion
  103.8 0.2 multiply_subtract_fusion.1
  103.9 0.4 fusion.35
  104.4 0.9 div.37
  (20 shorter events, 0.6 us)
Async XLA Ops:
  4.5 26.1 %all-to-all-start = ((f32[4,12,5,128]{3,0,2,1:T(4,128)}), f32[4,12,5,128]{3,0,2,1:T(4,128)S(1)}, u32[]{:S(2)}, u32[]{:S(2)}) async-start(f32[4,12,5,128]{3,0,2,1:T(4,128)} %pad_maximum_fusion.1), calls=%async_computation | async-start | bytes 245760 | tf_op jit(solution)/shard_map/all_to_all | solution.py:144
  39.9 30.7 %all-to-all-start.1 = ((bf16[64,2,2176]{2,1,0:T(2,128)(2,1)}), bf16[64,2,2176]{2,1,0:T(2,128)(2,1)S(1)}, u32[]{:S(2)}, u32[]{:S(2)}) async-start(bf16[64,2,2176]{2,1,0:T(2,128)(2,1)} %all_to_all.25), calls=%async_computation.1 | async-start | bytes 1114112 | tf_op jit(solution)/shard_map/all_to_all | solution.py:155

commit v4 on v3

--- a/solution.py
+++ b/solution.py
@@ -3,6 +3,8 @@
 import jax
 import jax.numpy as jnp
 from jax import lax
+from jax.experimental import pallas as pl
+from jax.experimental.pallas import tpu as pltpu
 from jax.sharding import PartitionSpec as P
 
 G = 2048
@@ -57,11 +59,11 @@
     col_side = jnp.einsum(
         "ikcx,cxn->ikn", jnp.stack([cos_v, sin_v], axis=2), table, precision=HIGH
     )
-    left = jnp.concatenate([row_side[:, :, :NS], row_side[:, :, NS:]], axis=1)
+    left = jnp.concatenate([col_side[:, :, :NS], col_side[:, :, NS:]], axis=1)
     right = jnp.concatenate(
-        [col_side, jnp.concatenate([-col_side[:, :, NS:], col_side[:, :, :NS]], axis=2)], axis=1
+        [row_side, jnp.concatenate([-row_side[:, :, NS:], row_side[:, :, :NS]], axis=2)], axis=1
     )
-    full = jnp.einsum("ikp,ikn->ipn", left, right, precision=HIGH)
+    full = jnp.einsum("ikq,ikn->iqn", left, right, precision=HIGH)
     return (full.reshape(count, NS, 2, NS) / (NS * NS)).astype(jnp.bfloat16)
 
 
@@ -72,19 +74,33 @@
     return owners * capacity + slot_rank
 
 
-def place_windows(windows, col_hi, col_lo, col_blocks):
-    slots = windows.shape[0]
-    wide = jnp.arange(2 * NS)
-    shift = (wide[None, None, :] == col_lo[:, None, None] + jnp.arange(NS)[None, :, None])
-    shifted = jnp.einsum(
-        "scpq,sqw->scpw", windows, shift.astype(jnp.bfloat16), preferred_element_type=jnp.float32
-    ).astype(jnp.bfloat16)
-    shifted = shifted.reshape(slots, 2, NS, 2, NS)
-    hit = jnp.arange(col_blocks)[:, None, None] == col_hi[None, :, None] + jnp.arange(2)[None, None, :]
-    grid = jnp.einsum(
-        "bsk,scpka->cpba", hit.astype(jnp.bfloat16), shifted, preferred_element_type=jnp.float32
-    )
-    return grid.reshape(2, NS, col_blocks * NS)
+def place_kernel(cols_ref, windows_ref, grid_ref):
+    grid_ref[...] = jnp.zeros(grid_ref.shape, grid_ref.dtype)
+    width = windows_ref.shape[1]
+
+    def add_slot(slot, carry):
+        start = cols_ref[slot]
+        grid_ref[pl.ds(start, width), :] += windows_ref[slot].astype(jnp.float32)
+        return carry
+
+    lax.fori_loop(0, windows_ref.shape[0], add_slot, 0, unroll=8)
+
+
+def place_slots(cols, windows):
+    slots, width, lanes = windows.shape
+    return pl.pallas_call(
+        place_kernel,
+        out_shape=jax.ShapeDtypeStruct((G, lanes), jnp.float32),
+        grid_spec=pltpu.PrefetchScalarGridSpec(
+            num_scalar_prefetch=1,
+            grid=(1,),
+            in_specs=[pl.BlockSpec((slots, width, lanes), lambda i, c: (0, 0, 0))],
+            out_specs=pl.BlockSpec((G, lanes), lambda i, c: (0, 0)),
+        ),
+        cost_estimate=pl.CostEstimate(
+            flops=slots * width * lanes, transcendentals=0, bytes_accessed=slots * width * lanes * 2 + G * lanes * 4
+        ),
+    )(cols, windows)
 
 
 def factor_lengths(length):
@@ -93,19 +109,18 @@
 
 
 def transform_rows(grid):
-    rows = grid.shape[1]
     outer_len, inner_len = factor_lengths(G)
-    split = grid.reshape(2, rows, inner_len, outer_len)
     first = block_matrix(*phase_table(inner_len, inner_len, inner_len, 1.0))
-    section = jnp.einsum("opba,Pobc->Pcpa", split, first, precision=HIGH)
+    section = jnp.einsum("baop,Pobc->caPp", grid, first, precision=HIGH)
     twiddle_real, twiddle_imag = phase_table(inner_len, outer_len, G, 1.0)
-    twiddle_real = twiddle_real[:, None, :]
-    twiddle_imag = twiddle_imag[:, None, :]
-    turned_real = section[0] * twiddle_real - section[1] * twiddle_imag
-    turned_imag = section[0] * twiddle_imag + section[1] * twiddle_real
-    turned = jnp.stack([turned_real, turned_imag])
+    twiddle_real = twiddle_real[:, :, None]
+    twiddle_imag = twiddle_imag[:, :, None]
+    section_real, section_imag = section[:, :, 0], section[:, :, 1]
+    turned_real = section_real * twiddle_real - section_imag * twiddle_imag
+    turned_imag = section_real * twiddle_imag + section_imag * twiddle_real
+    turned = jnp.stack([turned_real, turned_imag], axis=2)
     second = block_matrix(*phase_table(outer_len, outer_len, outer_len, 1.0))
-    return jnp.einsum("Ocpa,POad->dcPp", turned, second, precision=HIGH)
+    return jnp.einsum("caOp,POad->dcPp", turned, second, precision=HIGH)
 
 
 def transform_cols(turned):
@@ -118,7 +133,7 @@
     turned_real = section[0] * twiddle_real - section[1] * twiddle_imag
     turned_imag = section[0] * twiddle_imag + section[1] * twiddle_real
     second_real, second_imag = phase_table(outer_len, outer_len, outer_len, 1.0)
-    second = jnp.stack([second_real, -second_imag])
+    second = jnp.stack([second_real, -second_imag]) / G
     stacked = jnp.stack([turned_real, turned_imag])
     final = jnp.einsum("ocma,oad->mdc", stacked, second, precision=HIGH)
     return final.reshape(final.shape[0], G)
@@ -153,14 +168,15 @@
     pick = (jnp.arange(slot_count)[:, None] == target[None, :]).astype(jnp.bfloat16)
     outgoing = jnp.dot(pick, arrived, preferred_element_type=jnp.float32).astype(jnp.bfloat16)
     incoming = lax.all_to_all(outgoing, "tile", split_axis=0, concat_axis=0, tiled=True)
-    windows = incoming[:, :cell_count].reshape(slot_count, NS, 2, NS).transpose(0, 2, 1, 3)
+    windows = incoming[:, :cell_count].reshape(slot_count, NS, 2 * NS)
     col_hi = incoming[:, cell_count + 1].astype(jnp.int32)
     col_lo = incoming[:, cell_count + 2].astype(jnp.int32)
-    tile_grid = place_windows(windows, col_hi, col_lo, G // NS)
-    half = transform_rows(tile_grid)
+    cols = jnp.clip(col_hi * NS + col_lo, 0, G - NS)
+    tile_grid = place_slots(cols, windows)
+    half = transform_rows(tile_grid.reshape(G // NS, NS, 2, band_rows))
     half = half.reshape(tile_count, G // tile_count, 2, band_rows).astype(jnp.bfloat16)
     turned = lax.all_to_all(half, "tile", split_axis=0, concat_axis=0, tiled=True)
-    dirty_image = transform_cols(turned.astype(jnp.float32)) / G
+    dirty_image = transform_cols(turned.astype(jnp.float32))
     return dirty_image[None]
 
 

time: 106 us -> 108 us (1.019)
  Pallas kernels: 0 us -> 3.63 us
  matrix products: 8.07 us -> 6.13 us
    pallas_call x0 -> x1, Pallas kernels: none -> 3.63 us  [place_slots(): pl.pallas_call(place_kernel, out_shape=jax.ShapeDtypeStruct((G, lanes), j...]
    dot_general x5 -> x3, matrix products: 5.21 us -> 3.28 us  [the longest x1 1.5 us: form_subgrids(): full = jnp.einsum('ikq,ikn->iqn', left, right, precision=HIGH)]
    unnamed x4 -> x6, local copies, waits for them, and re-layouts: 2.4 us -> 2.57 us
    reshape x2 -> x3, local copies, waits for them, and re-layouts: 6.18 us -> 6.1 us  [the longest x2 3.59 us: per_device(): half = transform_rows(tile_grid.reshape(G // NS, NS, 2, band_rows))]
where the time goes in v4:
time: 108 us
  starting transfers between devices  28.4 us (26%)
  waiting for transfers between devices  27.7 us (26%)
  blocking collectives  18 us (17%)
  local copies, waits for them, and re-layouts  13.8 us (13%)
  other arithmetic  8.94 us (8%)
  matrix products  6.13 us (6%)
  Pallas kernels  3.63 us (3%)
    all_to_all x1, blocking collectives, per_device(): lax.all_to_all(half, 'tile', split_axis=0, concat_axis=0, tiled=True)  18 us
    all_to_all x1, waiting for transfers between devices, per_device(): lax.all_to_all(outgoing, 'tile', split_axis=0, concat_axis=0, tiled=True)  17.5 us
    all_to_all x1, starting transfers between devices, per_device(): lax.all_to_all(payload, 'chan', split_axis=1, concat_axis=0, tiled=True)  15.7 us
    all_to_all x1, starting transfers between devices, per_device(): lax.all_to_all(outgoing, 'tile', split_axis=0, concat_axis=0, tiled=True)  12.7 us
    all_to_all x1, waiting for transfers between devices, per_device(): lax.all_to_all(payload, 'chan', split_axis=1, concat_axis=0, tiled=True)  10.1 us
    pallas_call x1, Pallas kernels, place_slots(): pl.pallas_call(place_kernel, out_shape=jax.ShapeDtypeStruct((G, lanes), j...  3.63 us
    reshape x2, local copies, waits for them, and re-layouts, per_device(): half = transform_rows(tile_grid.reshape(G // NS, NS, 2, band_rows))  3.59 us
    unnamed x6, local copies, waits for them, and re-layouts  2.57 us
  transfers between devices with their start and end apart: 2, of which 2 were waited for; matrix products, arithmetic and copies ran while one was open for 1% of the time, Pallas kernels for 0%

profile of v4, /device:TPU:1, one launch (start us, length us, event | category | flops | bytes accessed | tf_op | source)
XLA Modules:
  0.0 107.6 jit_solution(4955132836231834253)
XLA Ops:
  0.0 0.7 and_select_fusion.1
  0.7 0.7 add_convert_fusion
  1.4 0.1 copy.77
  2.1 0.8 copy.84
  3.0 0.9 bitcast_multiply_fusion.4
  3.8 0.7 pad_maximum_fusion.1
  4.5 15.7 %all-to-all-start = ((f32[4,12,5,128]{3,0,2,1:T(4,128)}), f32[4,12,5,128]{3,0,2,1:T(4,128)S(1)}, u32[]{:S(2)}, u32[]{:S(2)}) async-start(f32[4,12,5,128]{3,0,2,1:T(4,128)} %pad_maximum_fusion.1), calls=%async_computation | async-start | bytes 245760 | tf_op jit(solution)/shard_map/all_to_all | solution.py:159
  20.3 0.1 fusion.88
  20.5 10.1 %all-to-all-done = f32[4,12,5,128]{3,0,2,1:T(4,128)S(1)} async-done(((f32[4,12,5,128]{3,0,2,1:T(4,128)}), f32[4,12,5,128]{3,0,2,1:T(4,128)S(1)}, u32[]{:S(2)}, u32[]{:S(2)}) %all-to-all-start) | async-done | bytes 122912 | tf_op jit(solution)/shard_map/all_to_all | solution.py:159
  30.7 1.6 %fusion.48 = (f32[48,128,4]{1,2,0:T(4,128)S(1)}, f32[48,128,4]{1,2,0:T(4,128)S(1)}, f32[48,128,4]{1,2,0:T(4,128)S(1)}, f32[48,128,4]{1,2,0:T(4,128)S(1)}) fusion(f32[4]{0:T(128)S(1)} %multiply_add_fusion.3, f32[48,128]{1,0:T(8,128)S(1)} %get-tuple-element.23, f32[48,128]{1,0:T(8,128)S(1)} %get-tuple-element.25), kind=kLoop, calls=%fused_computation.66 | loop fusion | flops 98304 | bytes 442384 | tf_op jit(solution)/shard_map/cos | solution.py:33
  32.3 1.5 %fusion.44 = (f32[48,128,8]{1,2,0:T(8,128)S(1)}, f32[48,128,8]{1,2,0:T(8,128)S(1)}, f32[48,128,8]{1,2,0:T(8,128)S(1)}, f32[48,128,8]{1,2,0:T(8,128)S(1)}) fusion(f32[8]{0:T(128)S(1)} %iota_convert_fusion, f32[48,128]{1,0:T(8,128)S(1)} %get-tuple-element.23, f32[48,128]{1,0:T(8,128)S(1)} %get-tuple-element.25), kind=kLoop, calls=%fused_computation.58 | loop fusion | flops 196608 | bytes 835616 | tf_op jit(solution)/shard_map/cos | solution.py:34
  33.7 0.2 subtract_bitcast_fusion
  34.0 0.8 fusion.20
  34.8 0.1 fusion.103
  34.9 0.4 fusion.31
  35.3 0.8 fusion.17
  36.1 0.2 slice_negate_fusion
  36.3 1.5 %multiply_convert_fusion = bf16[48,32,64]{2,1,0:T(8,128)(2,1)S(1)} fusion(f32[48,128,32]{1,2,0:T(8,128)S(1)} %get-tuple-element.12, f32[48,128,32]{1,2,0:T(8,128)S(1)} %get-tuple-element.11, f32[48,128,64]{1,2,0:T(8,128)S(1)} %fusion.17, f32[48,128,32]{1,2,0:T(8,128)S(1)} %get-tuple-element.10, f32[48,128,32]{1,2,0:T(8,128)S(1)} %get-tuple-element.9), kind=kOutput, calls=%fused_computation.40 | convolution fusion | flops 153157632 | bytes 4915200 | tf_op jit(solution)/shard_map/ikq,ikn->iqn/dot_general | solution.py:66
  37.8 0.4 convert_element_type.179
  38.2 0.1 convert_reduce_fusion
  38.4 0.2 select_reduce_fusion
  38.6 0.3 convolution_convert_fusion
  38.9 1.0 all_to_all.25
  39.9 12.7 %all-to-all-start.1 = ((bf16[64,2,2176]{2,1,0:T(2,128)(2,1)}), bf16[64,2,2176]{2,1,0:T(2,128)(2,1)S(1)}, u32[]{:S(2)}, u32[]{:S(2)}) async-start(bf16[64,2,2176]{2,1,0:T(2,128)(2,1)} %all_to_all.25), calls=%async_computation.1 | async-start | bytes 1114112 | tf_op jit(solution)/shard_map/all_to_all | solution.py:170
  52.7 0.1 fusion.84
  52.9 0.1 fusion.76
  53.1 17.5 %all-to-all-done.1 = bf16[64,2,2176]{2,1,0:T(2,128)(2,1)S(1)} async-done(((bf16[64,2,2176]{2,1,0:T(2,128)(2,1)}), bf16[64,2,2176]{2,1,0:T(2,128)(2,1)S(1)}, u32[]{:S(2)}, u32[]{:S(2)}) %all-to-all-start.1) | async-done | bytes 557088 | tf_op jit(solution)/shard_map/all_to_all | solution.py:170
  70.7 0.2 all_to_all.27
  71.0 0.3 copy.56
  71.3 2.5 %copy.57.windows_ref = bf16[128,32,64]{2,1,0:T(8,128)(2,1)} copy(bf16[128,32,64]{0,2,1:T(8,128)(2,1)S(1)} %bitcast.128) | data formatting | bytes 1048576 | tf_op jit(solution)/shard_map/reshape | solution.py:171
  73.9 0.1 copy.76
  74.0 0.5 clamp_bitcast_fusion.cols_ref
  74.6 3.6 %shard_map.55 = f32[2048,64]{1,0:T(8,128)} custom-call(s32[128]{0:T(128)} %clamp_bitcast_fusion.cols_ref, bf16[128,32,64]{2,1,0:T(8,128)(2,1)} %copy.57.windows_ref), custom_call_target="tpu_custom_call" | custom-call | flops 262144 | bytes 1048576 | tf_op jit(solution)/shard_map/pallas_call | solution.py:91
  78.2 2.5 %reshape.664 = f32[64,32,2,32]{3,2,1,0:T(2,128)S(1)} reshape(f32[2048,64]{1,0:T(8,128)} %shard_map.55) | data formatting | bytes 1048576 | tf_op jit(solution)/shard_map/reshape | solution.py:176
  80.7 1.1 %copy.59 = f32[64,32,2,32]{0,3,2,1:T(8,128)S(1)} copy(f32[64,32,2,32]{3,2,1,0:T(2,128)S(1)} %reshape.664) | data formatting | bytes 1048576 | tf_op jit(solution)/shard_map/reshape | solution.py:176
  81.8 0.6 convolution_bitcast_fusion.2
  82.5 0.2 multiply_subtract_fusion.2
  82.7 0.1 pad_maximum_fusion
  82.8 1.2 %fusion.24 = bf16[32,64,2,32]{1,0,3,2:T(8,128)(2,1)S(1)} fusion(f32[64,32,2,32]{0,3,1,2:T(8,128)S(1)} %pad_maximum_fusion, f32[1,2,32,32]{2,3,1,0:T(8,128)S(1)} %get-tuple-element.38, f32[1,2,32,32]{2,3,1,0:T(8,128)S(1)} %get-tuple-element.37), kind=kOutput, calls=%fused_computation.24 | convolution fusion | flops 50466816 | bytes 802816 | tf_op jit(solution)/shard_map/caOp,POad->dcPp/dot_general | solution.py:123
  83.9 0.9 copy.74
  84.8 1.0 reshape.667
  85.8 18.0 %all_to_all.32 = bf16[64,2,1024]{2,1,0:T(2,128)(2,1)S(1)} all-to-all(bf16[64,2,1024]{2,1,0:T(2,128)(2,1)S(1)} %reshape.667), channel_id=1, replica_groups=mesh['chan'=12,'tile'=64] {'tile'}, dimensions={0} | all-to-all | bytes 524288 | tf_op jit(solution)/shard_map/all_to_all | solution.py:178
  103.9 0.5 reshape.668
  104.4 1.2 %copy.62 = bf16[64,32,2,32]{0,3,2,1:T(8,128)(2,1)S(1)} copy(bf16[64,32,2,32]{3,2,1,0:T(2,128)(2,1)S(1)} %reshape.668) | data formatting | bytes 524288 | tf_op jit(solution)/shard_map/all_to_all | solution.py:178
  105.6 0.5 convolution_bitcast_fusion
  106.1 0.2 multiply_subtract_fusion.1
  106.2 0.4 convolution_bitcast_fusion.3
  106.7 0.9 broadcast_in_dim_reshape.3
  (22 shorter events, 0.9 us)
Async XLA Ops:
  4.5 26.1 %all-to-all-start = ((f32[4,12,5,128]{3,0,2,1:T(4,128)}), f32[4,12,5,128]{3,0,2,1:T(4,128)S(1)}, u32[]{:S(2)}, u32[]{:S(2)}) async-start(f32[4,12,5,128]{3,0,2,1:T(4,128)} %pad_maximum_fusion.1), calls=%async_computation | async-start | bytes 245760 | tf_op jit(solution)/shard_map/all_to_all | solution.py:159
  39.9 30.7 %all-to-all-start.1 = ((bf16[64,2,2176]{2,1,0:T(2,128)(2,1)}), bf16[64,2,2176]{2,1,0:T(2,128)(2,1)S(1)}, u32[]{:S(2)}, u32[]{:S(2)}) async-start(bf16[64,2,2176]{2,1,0:T(2,128)(2,1)} %all_to_all.25), calls=%async_computation.1 | async-start | bytes 1114112 | tf_op jit(solution)/shard_map/all_to_all | solution.py:170

commit v5 on v4

--- a/solution.py
+++ b/solution.py
@@ -74,33 +74,40 @@
     return owners * capacity + slot_rank
 
 
-def place_kernel(cols_ref, windows_ref, grid_ref):
+def place_kernel(cols_ref, tiles_ref, grid_ref):
     grid_ref[...] = jnp.zeros(grid_ref.shape, grid_ref.dtype)
-    width = windows_ref.shape[1]
-
-    def add_slot(slot, carry):
-        start = cols_ref[slot]
-        grid_ref[pl.ds(start, width), :] += windows_ref[slot].astype(jnp.float32)
+    width = 2 * NS
+
+    def add_source(source, carry):
+        for rank in range(2):
+            start = cols_ref[2 * source + rank]
+            window = tiles_ref[source, 0:NS, rank * width:(rank + 1) * width]
+            grid_ref[pl.ds(start, NS), :] += window.astype(jnp.float32)
         return carry
 
-    lax.fori_loop(0, windows_ref.shape[0], add_slot, 0, unroll=8)
-
-
-def place_slots(cols, windows):
-    slots, width, lanes = windows.shape
+    lax.fori_loop(0, tiles_ref.shape[0], add_source, 0, unroll=4)
+
+
+def place_slots(cols, tiles):
+    sources, rows, lanes = tiles.shape
     return pl.pallas_call(
         place_kernel,
-        out_shape=jax.ShapeDtypeStruct((G, lanes), jnp.float32),
+        out_shape=jax.ShapeDtypeStruct((G, lanes // 2), jnp.float32),
         grid_spec=pltpu.PrefetchScalarGridSpec(
             num_scalar_prefetch=1,
             grid=(1,),
-            in_specs=[pl.BlockSpec((slots, width, lanes), lambda i, c: (0, 0, 0))],
-            out_specs=pl.BlockSpec((G, lanes), lambda i, c: (0, 0)),
+            in_specs=[pl.BlockSpec((sources, rows, lanes), lambda i, c: (0, 0, 0))],
+            out_specs=pl.BlockSpec((G, lanes // 2), lambda i, c: (0, 0)),
         ),
         cost_estimate=pl.CostEstimate(
-            flops=slots * width * lanes, transcendentals=0, bytes_accessed=slots * width * lanes * 2 + G * lanes * 4
+            flops=sources * rows * lanes, transcendentals=0, bytes_accessed=sources * rows * lanes * 2 + G * lanes * 2
         ),
-    )(cols, windows)
+    )(cols, tiles)
+
+
+def times_i(x):
+    half = x.shape[-1] // 2
+    return jnp.concatenate([-x[..., half:], x[..., :half]], axis=-1)
 
 
 def factor_lengths(length):
@@ -110,17 +117,16 @@
 
 def transform_rows(grid):
     outer_len, inner_len = factor_lengths(G)
-    first = block_matrix(*phase_table(inner_len, inner_len, inner_len, 1.0))
-    section = jnp.einsum("baop,Pobc->caPp", grid, first, precision=HIGH)
+    first_real, first_imag = phase_table(inner_len, inner_len, inner_len, 1.0)
+    section = jnp.einsum("cb,ban->can", first_real, grid, precision=HIGH) + jnp.einsum(
+        "cb,ban->can", first_imag, times_i(grid), precision=HIGH
+    )
     twiddle_real, twiddle_imag = phase_table(inner_len, outer_len, G, 1.0)
-    twiddle_real = twiddle_real[:, :, None]
-    twiddle_imag = twiddle_imag[:, :, None]
-    section_real, section_imag = section[:, :, 0], section[:, :, 1]
-    turned_real = section_real * twiddle_real - section_imag * twiddle_imag
-    turned_imag = section_real * twiddle_imag + section_imag * twiddle_real
-    turned = jnp.stack([turned_real, turned_imag], axis=2)
-    second = block_matrix(*phase_table(outer_len, outer_len, outer_len, 1.0))
-    return jnp.einsum("caOp,POad->dcPp", turned, second, precision=HIGH)
+    turned = section * twiddle_real[:, :, None] + times_i(section) * twiddle_imag[:, :, None]
+    second_real, second_imag = phase_table(outer_len, outer_len, outer_len, 1.0)
+    return jnp.einsum("da,can->dcn", second_real, turned, precision=HIGH) + jnp.einsum(
+        "da,can->dcn", second_imag, times_i(turned), precision=HIGH
+    )
 
 
 def transform_cols(turned):
@@ -133,7 +139,7 @@
     turned_real = section[0] * twiddle_real - section[1] * twiddle_imag
     turned_imag = section[0] * twiddle_imag + section[1] * twiddle_real
     second_real, second_imag = phase_table(outer_len, outer_len, outer_len, 1.0)
-    second = jnp.stack([second_real, -second_imag]) / G
+    second = jnp.stack([second_real, -second_imag])
     stacked = jnp.stack([turned_real, turned_imag])
     final = jnp.einsum("ocma,oad->mdc", stacked, second, precision=HIGH)
     return final.reshape(final.shape[0], G)
@@ -167,16 +173,20 @@
     slot_count = tile_count * capacity
     pick = (jnp.arange(slot_count)[:, None] == target[None, :]).astype(jnp.bfloat16)
     outgoing = jnp.dot(pick, arrived, preferred_element_type=jnp.float32).astype(jnp.bfloat16)
-    incoming = lax.all_to_all(outgoing, "tile", split_axis=0, concat_axis=0, tiled=True)
-    windows = incoming[:, :cell_count].reshape(slot_count, NS, 2 * NS)
-    col_hi = incoming[:, cell_count + 1].astype(jnp.int32)
-    col_lo = incoming[:, cell_count + 2].astype(jnp.int32)
-    cols = jnp.clip(col_hi * NS + col_lo, 0, G - NS)
-    tile_grid = place_slots(cols, windows)
-    half = transform_rows(tile_grid.reshape(G // NS, NS, 2, band_rows))
+    lanes = 2 * NS
+    windows = outgoing[:, :cell_count].reshape(tile_count, capacity, NS, lanes)
+    windows = windows.transpose(0, 2, 1, 3).reshape(tile_count, NS, capacity * lanes)
+    where_to = outgoing[:, cell_count + 1:cell_count + 3].reshape(tile_count, capacity, 2)
+    where_to = jnp.pad(where_to, ((0, 0), (0, 0), (0, lanes - 2))).reshape(tile_count, 1, capacity * lanes)
+    tiles = jnp.concatenate([windows, where_to], axis=1)
+    incoming = lax.all_to_all(tiles, "tile", split_axis=0, concat_axis=0, tiled=True)
+    places = incoming[:, NS].reshape(tile_count, capacity, lanes)[:, :, 0:2].astype(jnp.int32)
+    cols = jnp.clip(places[:, :, 0] * NS + places[:, :, 1], 0, G - NS).reshape(slot_count)
+    tile_grid = place_slots(cols, incoming)
+    half = transform_rows(tile_grid.reshape(G // NS, NS, lanes))
     half = half.reshape(tile_count, G // tile_count, 2, band_rows).astype(jnp.bfloat16)
     turned = lax.all_to_all(half, "tile", split_axis=0, concat_axis=0, tiled=True)
-    dirty_image = transform_cols(turned.astype(jnp.float32))
+    dirty_image = transform_cols(turned.astype(jnp.float32)) / G
     return dirty_image[None]
 
 

time: 108 us -> 113 us (1.046)
  blocking collectives: 18 us -> 32.6 us
  starting transfers between devices: 28.4 us -> 22 us
  waiting for transfers between devices: 27.7 us -> 21.7 us
  other arithmetic: 8.94 us -> 10.3 us
    all_to_all x1, blocking collectives: 18 us -> 32.6 us  [per_device(): lax.all_to_all(tiles, 'tile', split_axis=0, concat_axis=0, tiled=True)]
    all_to_all x1, starting transfers between devices: 12.7 us -> 6.27 us  [per_device(): lax.all_to_all(half, 'tile', split_axis=0, concat_axis=0, tiled=True)]
    all_to_all x1, waiting for transfers between devices: 17.5 us -> 11.6 us  [per_device(): lax.all_to_all(half, 'tile', split_axis=0, concat_axis=0, tiled=True)]
    reshape x3 -> x5, local copies, waits for them, and re-layouts: 6.1 us -> 4.5 us  [the longest x2 2.15 us: per_device(): windows = outgoing[:, :cell_count].reshape(tile_count, capacity, NS, lanes)]
    unnamed x0 -> x2, matrix products: none -> 1.42 us
    all_to_all x2 -> x0, local copies, waits for them, and re-layouts: 1.23 us -> none  [per_device(): lax.all_to_all(outgoing, 'tile', split_axis=0, concat_axis=0, tiled=True)]
where the time goes in v5:
time: 113 us
  blocking collectives  32.6 us (29%)
  starting transfers between devices  22 us (19%)
  waiting for transfers between devices  21.7 us (19%)
  local copies, waits for them, and re-layouts  13.7 us (12%)
  other arithmetic  10.3 us (9%)
  matrix products  7.08 us (6%)
  Pallas kernels  4.5 us (4%)
    all_to_all x1, blocking collectives, per_device(): lax.all_to_all(tiles, 'tile', split_axis=0, concat_axis=0, tiled=True)  32.6 us
    all_to_all x1, starting transfers between devices, per_device(): lax.all_to_all(payload, 'chan', split_axis=1, concat_axis=0, tiled=True)  15.7 us
    all_to_all x1, waiting for transfers between devices, per_device(): lax.all_to_all(half, 'tile', split_axis=0, concat_axis=0, tiled=True)  11.6 us
    all_to_all x1, waiting for transfers between devices, per_device(): lax.all_to_all(payload, 'chan', split_axis=1, concat_axis=0, tiled=True)  10.1 us
    all_to_all x1, starting transfers between devices, per_device(): lax.all_to_all(half, 'tile', split_axis=0, concat_axis=0, tiled=True)  6.27 us
    pallas_call x1, Pallas kernels, place_slots(): pl.pallas_call(place_kernel, out_shape=jax.ShapeDtypeStruct((G, lanes //...  4.5 us
    unnamed x6, local copies, waits for them, and re-layouts  3.11 us
  transfers between devices with their start and end apart: 2, of which 2 were waited for; matrix products, arithmetic and copies ran while one was open for 1% of the time, Pallas kernels for 0%

profile of v5, /device:TPU:1, one launch (start us, length us, event | category | flops | bytes accessed | tf_op | source)
XLA Modules:
  0.0 112.9 jit_solution(14643607888919809717)
XLA Ops:
  0.7 0.7 and_select_fusion.1
  1.4 0.7 add_convert_fusion
  2.1 0.8 copy.73
  3.0 0.9 bitcast_multiply_fusion.4
  3.8 0.7 pad_maximum_fusion.3
  4.5 15.7 %all-to-all-start = ((f32[4,12,5,128]{3,0,2,1:T(4,128)}), f32[4,12,5,128]{3,0,2,1:T(4,128)S(1)}, u32[]{:S(2)}, u32[]{:S(2)}) async-start(f32[4,12,5,128]{3,0,2,1:T(4,128)} %pad_maximum_fusion.3), calls=%async_computation | async-start | bytes 245760 | tf_op jit(solution)/shard_map/all_to_all | solution.py:165
  20.5 10.1 %all-to-all-done = f32[4,12,5,128]{3,0,2,1:T(4,128)S(1)} async-done(((f32[4,12,5,128]{3,0,2,1:T(4,128)}), f32[4,12,5,128]{3,0,2,1:T(4,128)S(1)}, u32[]{:S(2)}, u32[]{:S(2)}) %all-to-all-start) | async-done | bytes 122912 | tf_op jit(solution)/shard_map/all_to_all | solution.py:165
  31.0 0.2 select_reduce_fusion
  31.1 1.6 %fusion.49 = (f32[48,128,4]{1,2,0:T(4,128)S(1)}, f32[48,128,4]{1,2,0:T(4,128)S(1)}, f32[48,128,4]{1,2,0:T(4,128)S(1)}, f32[48,128,4]{1,2,0:T(4,128)S(1)}) fusion(f32[4]{0:T(128)S(1)} %multiply_add_fusion.2, f32[48,128]{1,0:T(8,128)S(1)} %get-tuple-element.25, f32[48,128]{1,0:T(8,128)S(1)} %get-tuple-element.27), kind=kLoop, calls=%fused_computation.71 | loop fusion | flops 98304 | bytes 442384 | tf_op jit(solution)/shard_map/cos | solution.py:33
  32.7 1.5 %fusion.43 = (f32[48,128,8]{1,2,0:T(8,128)S(1)}, f32[48,128,8]{1,2,0:T(8,128)S(1)}, f32[48,128,8]{1,2,0:T(8,128)S(1)}, f32[48,128,8]{1,2,0:T(8,128)S(1)}) fusion(f32[8]{0:T(128)S(1)} %iota_convert_fusion, f32[48,128]{1,0:T(8,128)S(1)} %get-tuple-element.25, f32[48,128]{1,0:T(8,128)S(1)} %get-tuple-element.27), kind=kLoop, calls=%fused_computation.61 | loop fusion | flops 196608 | bytes 835616 | tf_op jit(solution)/shard_map/cos | solution.py:34
  34.2 0.2 subtract_bitcast_fusion
  34.4 0.8 fusion.20
  35.2 0.1 fusion.135
  35.4 0.3 fusion.30
  35.7 0.8 fusion.17
  36.6 0.2 slice_negate_fusion
  36.7 1.5 %multiply_convert_fusion = bf16[48,32,64]{2,1,0:T(8,128)(2,1)S(1)} fusion(f32[48,128,32]{1,2,0:T(8,128)S(1)} %get-tuple-element.12, f32[48,128,32]{1,2,0:T(8,128)S(1)} %get-tuple-element.11, f32[48,128,64]{1,2,0:T(8,128)S(1)} %fusion.17, f32[48,128,32]{1,2,0:T(8,128)S(1)} %get-tuple-element.10, f32[48,128,32]{1,2,0:T(8,128)S(1)} %get-tuple-element.9), kind=kOutput, calls=%fused_computation.41 | convolution fusion | flops 153157632 | bytes 4915200 | tf_op jit(solution)/shard_map/ikq,ikn->iqn/dot_general | solution.py:66
  38.2 0.4 convert_element_type.170
  38.6 0.3 convolution_convert_fusion
  39.2 1.1 reshape.662
  40.3 1.1 copy.72
  41.3 0.5 reshape.663
  41.9 32.6 %all_to_all.25.tiles_ref = bf16[64,33,128]{2,1,0:T(8,128)(2,1)S(1)} all-to-all(bf16[64,33,128]{2,1,0:T(8,128)(2,1)S(1)} %pad_maximum_fusion.2), channel_id=1, replica_groups=mesh['chan'=12,'tile'=64] {'tile'}, dimensions={0} | all-to-all | bytes 1081344 | tf_op jit(solution)/shard_map/all_to_all | solution.py:182
  74.7 1.2 %fusion.51 = s32[64,2]{1,0:T(8,128)S(1)} fusion(s32[64,2,2]{2,1,0:T(2,128)S(1)} %slice_convert_fusion), kind=kLoop, calls=%fused_computation.74 | loop fusion | flops 384 | bytes 1536 | tf_op jit(solution)/shard_map/jit(clip)/min | solution.py:184
  76.0 0.7 min.12.cols_ref
  76.7 4.5 %shard_map.55 = f32[2048,64]{1,0:T(8,128)} custom-call(s32[128]{0:T(128)} %min.12.cols_ref, bf16[64,33,128]{2,1,0:T(8,128)(2,1)} %copy-done), custom_call_target="tpu_custom_call" | custom-call | flops 270336 | bytes 1064960 | tf_op jit(solution)/shard_map/pallas_call | solution.py:93
  81.2 1.8 %copy.52 = f32[64,32,64]{0,2,1:T(8,128)S(1)} copy(f32[64,32,64]{2,1,0:T(8,128)} %bitcast.119) | data formatting | bytes 1048576 | tf_op jit(solution)/shard_map/reshape | solution.py:186
  83.1 0.7 fusion.65
  83.9 0.7 fusion.62
  84.6 0.2 add.208
  84.9 0.3 fusion.26
  85.2 0.9 copy.55
  86.2 0.6 fusion.84
  87.0 0.9 copy.56
  87.9 0.7 fusion.23
  88.6 0.2 copy.66
  88.8 0.4 reshape.683
  89.2 1.7 %reshape.688 = bf16[64,2,1024]{2,1,0:T(2,128)(2,1)} reshape(bf16[64,32,2,32]{3,2,1,0:T(2,128)(2,1)S(1)} %reshape.683) | data formatting | bytes 524288
  90.9 6.3 %all-to-all-start.2 = ((bf16[64,2,1024]{2,1,0:T(2,128)(2,1)}), bf16[64,2,1024]{2,1,0:T(2,128)(2,1)S(1)}, u32[]{:S(2)}, u32[]{:S(2)}) async-start(bf16[64,2,1024]{2,1,0:T(2,128)(2,1)} %reshape.688), calls=%async_computation.2 | async-start | bytes 524288 | tf_op jit(solution)/shard_map/all_to_all | solution.py:188
  97.2 0.1 fusion.103
  97.4 0.1 fusion.94
  97.6 11.6 %all-to-all-done.2 = bf16[64,2,1024]{2,1,0:T(2,128)(2,1)S(1)} async-done(((bf16[64,2,1024]{2,1,0:T(2,128)(2,1)}), bf16[64,2,1024]{2,1,0:T(2,128)(2,1)S(1)}, u32[]{:S(2)}, u32[]{:S(2)}) %all-to-all-start.2) | async-done | bytes 262176 | tf_op jit(solution)/shard_map/all_to_all | solution.py:188
  109.2 0.5 reshape.689
  109.7 1.2 %copy.59 = bf16[64,32,2,32]{0,3,2,1:T(8,128)(2,1)S(1)} copy(bf16[64,32,2,32]{3,2,1,0:T(2,128)(2,1)S(1)} %reshape.689) | data formatting | bytes 524288 | tf_op jit(solution)/shard_map/all_to_all | solution.py:188
  110.9 0.5 convolution_bitcast_fusion
  111.4 0.2 multiply_subtract_fusion.1
  111.6 0.4 fusion.25
  112.0 0.9 div.37
  (35 shorter events, 1.9 us)
Async XLA Ops:
  4.5 26.1 %all-to-all-start = ((f32[4,12,5,128]{3,0,2,1:T(4,128)}), f32[4,12,5,128]{3,0,2,1:T(4,128)S(1)}, u32[]{:S(2)}, u32[]{:S(2)}) async-start(f32[4,12,5,128]{3,0,2,1:T(4,128)} %pad_maximum_fusion.3), calls=%async_computation | async-start | bytes 245760 | tf_op jit(solution)/shard_map/all_to_all | solution.py:165
  74.5 2.2 %copy-start = (bf16[64,33,128]{2,1,0:T(8,128)(2,1)}, bf16[64,33,128]{2,1,0:T(8,128)(2,1)S(1)}, u32[]{:S(2)}) copy-start(bf16[64,33,128]{2,1,0:T(8,128)(2,1)S(1)} %all_to_all.25.tiles_ref) | copy-start | bytes 1622020
  90.9 18.3 %all-to-all-start.2 = ((bf16[64,2,1024]{2,1,0:T(2,128)(2,1)}), bf16[64,2,1024]{2,1,0:T(2,128)(2,1)S(1)}, u32[]{:S(2)}, u32[]{:S(2)}) async-start(bf16[64,2,1024]{2,1,0:T(2,128)(2,1)} %reshape.688), calls=%async_computation.2 | async-start | bytes 524288 | tf_op jit(solution)/shard_map/all_to_all | solution.py:188

commit v6 on v3

--- a/solution.py
+++ b/solution.py
@@ -118,7 +118,7 @@
     turned_real = section[0] * twiddle_real - section[1] * twiddle_imag
     turned_imag = section[0] * twiddle_imag + section[1] * twiddle_real
     second_real, second_imag = phase_table(outer_len, outer_len, outer_len, 1.0)
-    second = jnp.stack([second_real, -second_imag])
+    second = jnp.stack([second_real, -second_imag]) / G
     stacked = jnp.stack([turned_real, turned_imag])
     final = jnp.einsum("ocma,oad->mdc", stacked, second, precision=HIGH)
     return final.reshape(final.shape[0], G)
@@ -137,15 +137,19 @@
     masked = samples[0] * live_mask[:, None, None, None]
     owners = block_owner[0, :, 0]
     cols = placement_map[0, :, 1]
-    meta = jnp.stack([owners, cols // NS, cols % NS], axis=1).astype(jnp.float32)
-    meta = jnp.pad(meta, ((0, 0), (0, steps_time - 3)))
+    meta = jnp.stack([owners, cols], axis=1).astype(jnp.float32)
+    meta = jnp.pad(meta, ((0, 0), (0, steps_time - 2)))
     meta = jnp.broadcast_to(meta[:, None, None, :], (blocks, channels, 1, steps_time))
     payload = jnp.concatenate([masked, uv_coords[0], meta], axis=2)
     arrived = lax.all_to_all(payload, "chan", split_axis=1, concat_axis=0, tiled=True)
     arrived = arrived.reshape(group_blocks, 5, steps_time)
     formed = form_subgrids(arrived[:, 0:2], arrived[:, 2:4])
     cell_count = 2 * NS * NS
-    group_meta = arrived[:, 4, 0:META].astype(jnp.bfloat16)
+    group_cols = arrived[:, 4, 1]
+    col_hi = jnp.floor(group_cols / NS)
+    col_lo = group_cols - NS * col_hi
+    group_meta = jnp.stack([arrived[:, 4, 0], col_hi, col_lo], axis=1)
+    group_meta = jnp.pad(group_meta, ((0, 0), (0, META - 3))).astype(jnp.bfloat16)
     arrived = jnp.concatenate([formed.reshape(group_blocks, cell_count), group_meta], axis=1)
     group_owners = group_meta[:, 0].astype(jnp.int32)
     target = slot_targets(group_owners, tile_count, capacity)
@@ -160,7 +164,7 @@
     half = transform_rows(tile_grid)
     half = half.reshape(tile_count, G // tile_count, 2, band_rows).astype(jnp.bfloat16)
     turned = lax.all_to_all(half, "tile", split_axis=0, concat_axis=0, tiled=True)
-    dirty_image = transform_cols(turned.astype(jnp.float32)) / G
+    dirty_image = transform_cols(turned.astype(jnp.float32))
     return dirty_image[None]
 
 

time: 106 us -> 106 us (level)
    another operation x0 -> x2, local copies, waits for them, and re-layouts: none -> 1.57 us  [the longest x1 0.89 us: per_device(): return dirty_image[None]]
    unnamed x4 -> x5, local copies, waits for them, and re-layouts: 2.4 us -> 2.51 us
where the time goes in v6:
time: 106 us
  starting transfers between devices  28.4 us (27%)
  waiting for transfers between devices  27.6 us (26%)
  blocking collectives  18 us (17%)
  local copies, waits for them, and re-layouts  14.7 us (14%)
  matrix products  8.08 us (8%)
  other arithmetic  7.85 us (7%)
    all_to_all x1, blocking collectives, per_device(): lax.all_to_all(half, 'tile', split_axis=0, concat_axis=0, tiled=True)  18 us
    all_to_all x1, waiting for transfers between devices, per_device(): lax.all_to_all(outgoing, 'tile', split_axis=0, concat_axis=0, tiled=True)  17.4 us
    all_to_all x1, starting transfers between devices, per_device(): lax.all_to_all(payload, 'chan', split_axis=1, concat_axis=0, tiled=True)  15.7 us
    all_to_all x1, starting transfers between devices, per_device(): lax.all_to_all(outgoing, 'tile', split_axis=0, concat_axis=0, tiled=True)  12.7 us
    all_to_all x1, waiting for transfers between devices, per_device(): lax.all_to_all(payload, 'chan', split_axis=1, concat_axis=0, tiled=True)  10.1 us
    reshape x1, local copies, waits for them, and re-layouts, place_windows(): shifted = shifted.reshape(slots, 2, NS, 2, NS)  3.2 us
    reshape x1, local copies, waits for them, and re-layouts, per_device(): incoming[:, :cell_count].reshape(slot_count, NS, 2, NS)  2.98 us
    unnamed x5, local copies, waits for them, and re-layouts  2.51 us
  transfers between devices with their start and end apart: 2, of which 2 were waited for; matrix products, arithmetic and copies ran while one was open for 1% of the time, Pallas kernels for 0%

profile of v6, /device:TPU:1, one launch (start us, length us, event | category | flops | bytes accessed | tf_op | source)
XLA Modules:
  0.0 105.7 jit_solution(6302437203614123341)
XLA Ops:
  0.7 0.8 copy.70
  1.5 0.7 slice_bitcast_fusion.4
  2.2 0.7 add_convert_fusion
  2.8 0.1 copy.62
  2.9 0.9 bitcast_multiply_fusion.4
  3.8 0.7 pad_maximum_fusion.1
  4.5 15.7 %all-to-all-start = ((f32[4,12,5,128]{3,0,2,1:T(4,128)}), f32[4,12,5,128]{3,0,2,1:T(4,128)S(1)}, u32[]{:S(2)}, u32[]{:S(2)}) async-start(f32[4,12,5,128]{3,0,2,1:T(4,128)} %pad_maximum_fusion.1), calls=%async_computation | async-start | bytes 245760 | tf_op jit(solution)/shard_map/all_to_all | solution.py:144
  20.5 10.1 %all-to-all-done = f32[4,12,5,128]{3,0,2,1:T(4,128)S(1)} async-done(((f32[4,12,5,128]{3,0,2,1:T(4,128)}), f32[4,12,5,128]{3,0,2,1:T(4,128)S(1)}, u32[]{:S(2)}, u32[]{:S(2)}) %all-to-all-start) | async-done | bytes 122912 | tf_op jit(solution)/shard_map/all_to_all | solution.py:144
  30.7 0.1 convert_reduce_fusion.2
  30.8 0.1 fusion.108
  30.9 0.2 slice_reduce_fusion
  31.1 1.5 %fusion.56 = (f32[48,128,8]{1,2,0:T(8,128)S(1)}, f32[48,128,8]{1,2,0:T(8,128)S(1)}, f32[48,128,8]{1,2,0:T(8,128)S(1)}, f32[48,128,8]{1,2,0:T(8,128)S(1)}) fusion(f32[8]{0:T(128)S(1)} %iota_convert_fusion, f32[48,128]{1,0:T(8,128)S(1)} %get-tuple-element.22, f32[48,128]{1,0:T(8,128)S(1)} %get-tuple-element.20), kind=kLoop, calls=%fused_computation.67 | loop fusion | flops 196608 | bytes 835616 | tf_op jit(solution)/shard_map/cos | solution.py:32
  32.5 1.6 %fusion.61 = (f32[48,128,4]{1,2,0:T(4,128)S(1)}, f32[48,128,4]{1,2,0:T(4,128)S(1)}, f32[48,128,4]{1,2,0:T(4,128)S(1)}, f32[48,128,4]{1,2,0:T(4,128)S(1)}) fusion(f32[4]{0:T(128)S(1)} %multiply_add_fusion.3, f32[48,128]{1,0:T(8,128)S(1)} %get-tuple-element.22, f32[48,128]{1,0:T(8,128)S(1)} %get-tuple-element.20), kind=kLoop, calls=%fused_computation.76 | loop fusion | flops 98304 | bytes 442384 | tf_op jit(solution)/shard_map/cos | solution.py:31
  34.1 0.3 fusion.40
  34.4 0.8 fusion.29
  35.3 0.1 fusion.123
  35.4 0.2 subtract_bitcast_fusion
  35.7 0.8 fusion.26
  36.5 0.2 slice_negate_fusion
  36.7 1.5 %multiply_convert_fusion = bf16[48,32,64]{2,1,0:T(8,128)(2,1)S(1)} fusion(f32[48,128,32]{1,2,0:T(8,128)S(1)} %get-tuple-element.10, f32[48,128,32]{1,2,0:T(8,128)S(1)} %get-tuple-element.9, f32[48,128,64]{1,2,0:T(8,128)S(1)} %fusion.26, f32[48,128,32]{1,2,0:T(8,128)S(1)} %get-tuple-element.8, f32[48,128,32]{1,2,0:T(8,128)S(1)} %get-tuple-element.7), kind=kOutput, calls=%fused_computation.46 | convolution fusion | flops 153157632 | bytes 4915200 | tf_op jit(solution)/shard_map/ikp,ikn->ipn/dot_general | solution.py:64
  38.2 0.4 convert_element_type.187
  38.7 0.2 select_reduce_fusion
  38.9 0.1 copy.63
  39.0 0.3 convolution_convert_fusion
  39.3 1.0 all_to_all.25
  40.3 12.7 %all-to-all-start.1 = ((bf16[64,2,2176]{2,1,0:T(2,128)(2,1)}), bf16[64,2,2176]{2,1,0:T(2,128)(2,1)S(1)}, u32[]{:S(2)}, u32[]{:S(2)}) async-start(bf16[64,2,2176]{2,1,0:T(2,128)(2,1)} %all_to_all.25), calls=%async_computation.1 | async-start | bytes 1114112 | tf_op jit(solution)/shard_map/all_to_all | solution.py:159
  53.1 0.1 fusion.99
  53.4 0.1 fusion.91
  53.6 17.4 %all-to-all-done.1 = bf16[64,2,2176]{2,1,0:T(2,128)(2,1)S(1)} async-done(((bf16[64,2,2176]{2,1,0:T(2,128)(2,1)}), bf16[64,2,2176]{2,1,0:T(2,128)(2,1)S(1)}, u32[]{:S(2)}, u32[]{:S(2)}) %all-to-all-start.1) | async-done | bytes 557088 | tf_op jit(solution)/shard_map/all_to_all | solution.py:159
  71.1 0.2 all_to_all.27
  71.3 0.2 convert_reduce_fusion
  71.5 0.3 copy.42
  71.8 3.0 %copy.43 = bf16[128,32,2,32]{3,1,2,0:T(8,128)(2,1)S(1)} copy(bf16[128,32,2,32]{0,3,2,1:T(8,128)(2,1)S(1)} %bitcast.151) | data formatting | bytes 1048576 | tf_op jit(solution)/shard_map/reshape | solution.py:160
  74.9 2.0 %fusion.10 = bf16[128,2,32,64]{3,2,1,0:T(8,128)(2,1)} fusion(bf16[128,32,2,32]{3,1,2,0:T(8,128)(2,1)S(1)} %copy.43, s32[128,32]{1,0:T(8,128)S(1)} %iota_add_fusion), kind=kOutput, calls=%fused_computation.11 | convolution fusion | flops 34340864 | bytes 1589248 | tf_op jit(solution)/shard_map/scpq,sqw->scpw/dot_general | solution.py:79
  76.9 3.2 %copy.60 = bf16[128,2,32,64]{0,3,1,2:T(8,128)(2,1)S(1)} copy(bf16[128,2,32,64]{3,2,1,0:T(8,128)(2,1)} %fusion.10) | data formatting | bytes 2097152 | tf_op jit(solution)/shard_map/reshape | solution.py:82
  80.1 0.4 convolution_bitcast_fusion.3
  80.6 0.6 convolution_bitcast_fusion.2
  81.2 0.2 multiply_subtract_fusion.2
  81.4 0.6 fusion.33
  82.0 0.9 copy.61
  82.9 1.0 reshape.618
  83.9 18.0 %all_to_all.32 = bf16[64,2,1024]{2,1,0:T(2,128)(2,1)S(1)} all-to-all(bf16[64,2,1024]{2,1,0:T(2,128)(2,1)S(1)} %reshape.618), channel_id=1, replica_groups=mesh['chan'=12,'tile'=64] {'tile'}, dimensions={0} | all-to-all | bytes 524288 | tf_op jit(solution)/shard_map/all_to_all | solution.py:166
  102.0 0.5 reshape.619
  102.5 1.2 %copy.48 = bf16[64,32,2,32]{0,3,2,1:T(8,128)(2,1)S(1)} copy(bf16[64,32,2,32]{3,2,1,0:T(2,128)(2,1)S(1)} %reshape.619) | data formatting | bytes 524288 | tf_op jit(solution)/shard_map/all_to_all | solution.py:166
  103.7 0.5 convolution_bitcast_fusion
  104.2 0.2 multiply_subtract_fusion.1
  104.3 0.4 convolution_bitcast_fusion.4
  104.8 0.9 broadcast_in_dim_reshape.3
  (23 shorter events, 0.9 us)
Async XLA Ops:
  4.5 26.1 %all-to-all-start = ((f32[4,12,5,128]{3,0,2,1:T(4,128)}), f32[4,12,5,128]{3,0,2,1:T(4,128)S(1)}, u32[]{:S(2)}, u32[]{:S(2)}) async-start(f32[4,12,5,128]{3,0,2,1:T(4,128)} %pad_maximum_fusion.1), calls=%async_computation | async-start | bytes 245760 | tf_op jit(solution)/shard_map/all_to_all | solution.py:144
  40.3 30.7 %all-to-all-start.1 = ((bf16[64,2,2176]{2,1,0:T(2,128)(2,1)}), bf16[64,2,2176]{2,1,0:T(2,128)(2,1)S(1)}, u32[]{:S(2)}, u32[]{:S(2)}) async-start(bf16[64,2,2176]{2,1,0:T(2,128)(2,1)} %all_to_all.25), calls=%async_computation.1 | async-start | bytes 1114112 | tf_op jit(solution)/shard_map/all_to_all | solution.py:159

commit v7 on v3

--- a/solution.py
+++ b/solution.py
@@ -22,16 +22,29 @@
     return jnp.stack([jnp.stack([real, -imag]), jnp.stack([imag, real])])
 
 
+def complex_product(left, right):
+    return (left[0] * right[0] - left[1] * right[1], left[0] * right[1] + left[1] * right[0])
+
+
+def bit_select(bits, value):
+    return (jnp.where(bits, value[0], 1.0), jnp.where(bits, value[1], 0.0))
+
+
 def offset_phase(coord):
-    factor = 2.0 * math.pi / NS
-    coarse = (8.0 * jnp.arange(4) - NS / 2.0).astype(jnp.float32)
-    fine = jnp.arange(8).astype(jnp.float32)
-    angle_c = coord[..., None] * coarse * factor
-    angle_f = coord[..., None] * fine * factor
-    cos_c, sin_c = jnp.cos(angle_c)[..., :, None], jnp.sin(angle_c)[..., :, None]
-    cos_f, sin_f = jnp.cos(angle_f)[..., None, :], jnp.sin(angle_f)[..., None, :]
-    real = cos_c * cos_f - sin_c * sin_f
-    imag = sin_c * cos_f + cos_c * sin_f
+    theta = coord * (2.0 * math.pi / NS)
+    squares = [(jnp.cos(theta)[..., None], jnp.sin(theta)[..., None])]
+    for _ in range(4):
+        squares.append(complex_product(squares[-1], squares[-1]))
+    fine_index = jnp.arange(8)
+    fine = bit_select((fine_index & 1) > 0, squares[0])
+    fine = complex_product(fine, bit_select((fine_index & 2) > 0, squares[1]))
+    fine = complex_product(fine, bit_select((fine_index & 4) > 0, squares[2]))
+    coarse_index = jnp.arange(4)
+    start = (squares[4][0], -squares[4][1])
+    coarse = complex_product(start, bit_select((coarse_index & 1) > 0, squares[3]))
+    coarse = complex_product(coarse, bit_select((coarse_index & 2) > 0, squares[4]))
+    real = coarse[0][..., :, None] * fine[0][..., None, :] - coarse[1][..., :, None] * fine[1][..., None, :]
+    imag = coarse[1][..., :, None] * fine[0][..., None, :] + coarse[0][..., :, None] * fine[1][..., None, :]
     shape = coord.shape + (NS,)
     return real.reshape(shape), imag.reshape(shape)
 

time: 106 us -> 104 us (0.981)
  other arithmetic: 8.54 us -> 6.54 us
    cos x2 -> x0, other arithmetic: 3.02 us -> none  [the longest x1 1.57 us: offset_phase(): jnp.cos(angle_c)[..., :, None]]
where the time goes in v7:
time: 104 us; the launch traced here: 103 us
  starting transfers between devices  28.4 us (27%)
  waiting for transfers between devices  27.6 us (27%)
  blocking collectives  18 us (17%)
  local copies, waits for them, and re-layouts  13.6 us (13%)
  matrix products  8.07 us (8%)
  other arithmetic  6.54 us (6%)
    all_to_all x1, blocking collectives, per_device(): lax.all_to_all(half, 'tile', split_axis=0, concat_axis=0, tiled=True)  18 us
    all_to_all x1, waiting for transfers between devices, per_device(): lax.all_to_all(outgoing, 'tile', split_axis=0, concat_axis=0, tiled=True)  17.4 us
    all_to_all x1, starting transfers between devices, per_device(): lax.all_to_all(payload, 'chan', split_axis=1, concat_axis=0, tiled=True)  15.7 us
    all_to_all x1, starting transfers between devices, per_device(): lax.all_to_all(outgoing, 'tile', split_axis=0, concat_axis=0, tiled=True)  12.7 us
    all_to_all x1, waiting for transfers between devices, per_device(): lax.all_to_all(payload, 'chan', split_axis=1, concat_axis=0, tiled=True)  10.1 us
    reshape x1, local copies, waits for them, and re-layouts, place_windows(): shifted = shifted.reshape(slots, 2, NS, 2, NS)  3.2 us
    reshape x1, local copies, waits for them, and re-layouts, per_device(): incoming[:, :cell_count].reshape(slot_count, NS, 2, NS)  2.98 us
    unnamed x4, local copies, waits for them, and re-layouts  2.4 us
  transfers between devices with their start and end apart: 2, of which 2 were waited for; matrix products, arithmetic and copies ran while one was open for 1% of the time, Pallas kernels for 0%

profile of v7, /device:TPU:1, one launch (start us, length us, event | category | flops | bytes accessed | tf_op | source)
XLA Modules:
  0.0 103.2 jit_solution(13744706927908016589)
XLA Ops:
  0.0 0.7 and_select_fusion.1
  0.7 0.7 add_convert_fusion
  1.4 0.1 copy.77
  2.1 0.8 copy.84
  3.0 0.9 bitcast_multiply_fusion.4
  3.8 0.7 pad_maximum_fusion.1
  4.5 15.7 %all-to-all-start = ((f32[4,12,5,128]{3,0,2,1:T(4,128)}), f32[4,12,5,128]{3,0,2,1:T(4,128)S(1)}, u32[]{:S(2)}, u32[]{:S(2)}) async-start(f32[4,12,5,128]{3,0,2,1:T(4,128)} %pad_maximum_fusion.1), calls=%async_computation | async-start | bytes 245760 | tf_op jit(solution)/shard_map/all_to_all | solution.py:157
  20.4 0.1 fusion.108
  20.5 10.1 %all-to-all-done = f32[4,12,5,128]{3,0,2,1:T(4,128)S(1)} async-done(((f32[4,12,5,128]{3,0,2,1:T(4,128)}), f32[4,12,5,128]{3,0,2,1:T(4,128)S(1)}, u32[]{:S(2)}, u32[]{:S(2)}) %all-to-all-start) | async-done | bytes 122912 | tf_op jit(solution)/shard_map/all_to_all | solution.py:157
  30.7 0.2 multiply_subtract_fusion.7
  30.9 0.2 slice_bitcast_fusion.1
  31.1 0.3 fusion.62
  31.4 0.3 fusion.54
  31.7 0.3 fusion.42
  32.0 0.8 fusion.29
  32.9 0.1 fusion.124
  33.0 0.2 subtract_bitcast_fusion
  33.3 0.8 fusion.26
  34.1 0.2 slice_negate_fusion
  34.3 1.5 %multiply_convert_fusion = bf16[48,32,64]{2,1,0:T(8,128)(2,1)S(1)} fusion(f32[48,128,32]{1,2,0:T(8,128)S(1)} %get-tuple-element.24, f32[48,128,32]{1,2,0:T(8,128)S(1)} %get-tuple-element.23, f32[48,128,64]{1,2,0:T(8,128)S(1)} %fusion.26, f32[48,128,32]{1,2,0:T(8,128)S(1)} %get-tuple-element.22, f32[48,128,32]{1,2,0:T(8,128)S(1)} %get-tuple-element.21), kind=kOutput, calls=%fused_computation.48 | convolution fusion | flops 153157632 | bytes 4915200 | tf_op jit(solution)/shard_map/ikp,ikn->ipn/dot_general | solution.py:77
  35.8 0.4 convert_element_type.167
  36.1 0.1 convert_reduce_fusion.2
  36.4 0.2 select_reduce_fusion
  36.6 0.3 convolution_convert_fusion
  36.9 1.0 all_to_all.25
  37.9 12.7 %all-to-all-start.1 = ((bf16[64,2,2176]{2,1,0:T(2,128)(2,1)}), bf16[64,2,2176]{2,1,0:T(2,128)(2,1)S(1)}, u32[]{:S(2)}, u32[]{:S(2)}) async-start(bf16[64,2,2176]{2,1,0:T(2,128)(2,1)} %all_to_all.25), calls=%async_computation.1 | async-start | bytes 1114112 | tf_op jit(solution)/shard_map/all_to_all | solution.py:168
  50.7 0.1 fusion.104
  51.0 0.1 fusion.97
  51.2 17.4 %all-to-all-done.1 = bf16[64,2,2176]{2,1,0:T(2,128)(2,1)S(1)} async-done(((bf16[64,2,2176]{2,1,0:T(2,128)(2,1)}), bf16[64,2,2176]{2,1,0:T(2,128)(2,1)S(1)}, u32[]{:S(2)}, u32[]{:S(2)}) %all-to-all-start.1) | async-done | bytes 557088 | tf_op jit(solution)/shard_map/all_to_all | solution.py:168
  68.6 0.2 all_to_all.27
  68.9 0.2 convert_reduce_fusion
  69.1 0.3 copy.57
  69.4 3.0 %copy.58 = bf16[128,32,2,32]{3,1,2,0:T(8,128)(2,1)S(1)} copy(bf16[128,32,2,32]{0,3,2,1:T(8,128)(2,1)S(1)} %bitcast.260) | data formatting | bytes 1048576 | tf_op jit(solution)/shard_map/reshape | solution.py:169
  72.4 2.0 %fusion.10 = bf16[128,2,32,64]{3,2,1,0:T(8,128)(2,1)} fusion(bf16[128,32,2,32]{3,1,2,0:T(8,128)(2,1)S(1)} %copy.58, s32[128,32]{1,0:T(8,128)S(1)} %iota_add_fusion), kind=kOutput, calls=%fused_computation.11 | convolution fusion | flops 34340864 | bytes 1589248 | tf_op jit(solution)/shard_map/scpq,sqw->scpw/dot_general | solution.py:92
  74.5 3.2 %copy.75 = bf16[128,2,32,64]{0,3,1,2:T(8,128)(2,1)S(1)} copy(bf16[128,2,32,64]{3,2,1,0:T(8,128)(2,1)} %fusion.10) | data formatting | bytes 2097152 | tf_op jit(solution)/shard_map/reshape | solution.py:95
  77.7 0.4 convolution_bitcast_fusion.3
  78.1 0.6 convolution_bitcast_fusion.2
  78.8 0.2 multiply_subtract_fusion.2
  78.9 0.6 fusion.33
  79.6 0.9 copy.76
  80.5 1.0 reshape.909
  81.5 18.0 %all_to_all.32 = bf16[64,2,1024]{2,1,0:T(2,128)(2,1)S(1)} all-to-all(bf16[64,2,1024]{2,1,0:T(2,128)(2,1)S(1)} %reshape.909), channel_id=1, replica_groups=mesh['chan'=12,'tile'=64] {'tile'}, dimensions={0} | all-to-all | bytes 524288 | tf_op jit(solution)/shard_map/all_to_all | solution.py:175
  99.5 0.5 reshape.910
  100.0 1.2 %copy.63 = bf16[64,32,2,32]{0,3,2,1:T(8,128)(2,1)S(1)} copy(bf16[64,32,2,32]{3,2,1,0:T(2,128)(2,1)S(1)} %reshape.910) | data formatting | bytes 524288 | tf_op jit(solution)/shard_map/all_to_all | solution.py:175
  101.2 0.5 convolution_bitcast_fusion
  101.7 0.2 multiply_subtract_fusion.1
  101.9 0.4 fusion.35
  102.3 0.9 div.37
  (23 shorter events, 0.8 us)
Async XLA Ops:
  4.5 26.1 %all-to-all-start = ((f32[4,12,5,128]{3,0,2,1:T(4,128)}), f32[4,12,5,128]{3,0,2,1:T(4,128)S(1)}, u32[]{:S(2)}, u32[]{:S(2)}) async-start(f32[4,12,5,128]{3,0,2,1:T(4,128)} %pad_maximum_fusion.1), calls=%async_computation | async-start | bytes 245760 | tf_op jit(solution)/shard_map/all_to_all | solution.py:157
  37.9 30.7 %all-to-all-start.1 = ((bf16[64,2,2176]{2,1,0:T(2,128)(2,1)}), bf16[64,2,2176]{2,1,0:T(2,128)(2,1)S(1)}, u32[]{:S(2)}, u32[]{:S(2)}) async-start(bf16[64,2,2176]{2,1,0:T(2,128)(2,1)} %all_to_all.25), calls=%async_computation.1 | async-start | bytes 1114112 | tf_op jit(solution)/shard_map/all_to_all | solution.py:168

commit v8 on v7

--- a/solution.py
+++ b/solution.py
@@ -64,12 +64,12 @@
             jnp.concatenate([-table_imag, table_real], axis=1),
         ]
     )
-    row_side = jnp.einsum(
-        "ikcx,cxn->ikn", jnp.stack([weight_real, weight_imag], axis=2), table, precision=HIGH
+    steps_time = masked.shape[-1]
+    both = jnp.concatenate(
+        [jnp.stack([weight_real, weight_imag], axis=2), jnp.stack([cos_v, sin_v], axis=2)], axis=1
     )
-    col_side = jnp.einsum(
-        "ikcx,cxn->ikn", jnp.stack([cos_v, sin_v], axis=2), table, precision=HIGH
-    )
+    both = jnp.einsum("ikcx,cxn->ikn", both, table, precision=HIGH)
+    row_side, col_side = both[:, :steps_time], both[:, steps_time:]
     left = jnp.concatenate([row_side[:, :, :NS], row_side[:, :, NS:]], axis=1)
     right = jnp.concatenate(
         [col_side, jnp.concatenate([-col_side[:, :, NS:], col_side[:, :, :NS]], axis=2)], axis=1
@@ -171,8 +171,9 @@
     col_lo = incoming[:, cell_count + 2].astype(jnp.int32)
     tile_grid = place_windows(windows, col_hi, col_lo, G // NS)
     half = transform_rows(tile_grid)
-    half = half.reshape(tile_count, G // tile_count, 2, band_rows).astype(jnp.bfloat16)
+    half = half.astype(jnp.bfloat16).reshape(tile_count, 2, G * band_rows // tile_count)
     turned = lax.all_to_all(half, "tile", split_axis=0, concat_axis=0, tiled=True)
+    turned = turned.reshape(tile_count, G // tile_count, 2, band_rows)
     dirty_image = transform_cols(turned.astype(jnp.float32)) / G
     return dirty_image[None]
 

time: 104 us -> 102 us (0.981)
  local copies, waits for them, and re-layouts: 13.6 us -> 12.3 us
    unnamed x4 -> x2, local copies, waits for them, and re-layouts: 2.4 us -> 0.91 us
where the time goes in v8:
time: 102 us
  starting transfers between devices  28.4 us (28%)
  waiting for transfers between devices  27.6 us (27%)
  blocking collectives  18 us (18%)
  local copies, waits for them, and re-layouts  12.3 us (12%)
  matrix products  7.91 us (8%)
  other arithmetic  6.79 us (7%)
    all_to_all x1, blocking collectives, per_device(): lax.all_to_all(half, 'tile', split_axis=0, concat_axis=0, tiled=True)  18 us
    all_to_all x1, waiting for transfers between devices, per_device(): lax.all_to_all(outgoing, 'tile', split_axis=0, concat_axis=0, tiled=True)  17.4 us
    all_to_all x1, starting transfers between devices, per_device(): lax.all_to_all(payload, 'chan', split_axis=1, concat_axis=0, tiled=True)  15.7 us
    all_to_all x1, starting transfers between devices, per_device(): lax.all_to_all(outgoing, 'tile', split_axis=0, concat_axis=0, tiled=True)  12.7 us
    all_to_all x1, waiting for transfers between devices, per_device(): lax.all_to_all(payload, 'chan', split_axis=1, concat_axis=0, tiled=True)  10.1 us
    reshape x1, local copies, waits for them, and re-layouts, place_windows(): shifted = shifted.reshape(slots, 2, NS, 2, NS)  3.2 us
    reshape x1, local copies, waits for them, and re-layouts, per_device(): incoming[:, :cell_count].reshape(slot_count, NS, 2, NS)  2.98 us
    dot_general x1, matrix products, place_windows(): jnp.einsum('scpq,sqw->scpw', windows, shift.astype(jnp.bfloat16), preferr...  2.05 us
  transfers between devices with their start and end apart: 2, of which 2 were waited for; matrix products, arithmetic and copies ran while one was open for 1% of the time, Pallas kernels for 0%

profile of v8, /device:TPU:1, one launch (start us, length us, event | category | flops | bytes accessed | tf_op | source)
XLA Modules:
  0.0 101.9 jit_solution(5865715389863054444)
XLA Ops:
  0.0 0.7 and_select_fusion.1
  0.7 0.7 add_convert_fusion
  1.4 0.1 copy.76
  1.5 0.8 copy.83
  2.9 0.9 bitcast_multiply_fusion.4
  3.8 0.7 pad_maximum_fusion.1
  4.5 15.7 %all-to-all-start = ((f32[4,12,5,128]{3,0,2,1:T(4,128)}), f32[4,12,5,128]{3,0,2,1:T(4,128)S(1)}, u32[]{:S(2)}, u32[]{:S(2)}) async-start(f32[4,12,5,128]{3,0,2,1:T(4,128)} %pad_maximum_fusion.1), calls=%async_computation | async-start | bytes 245760 | tf_op jit(solution)/shard_map/all_to_all | solution.py:157
  20.3 0.1 fusion.106
  20.5 10.1 %all-to-all-done = f32[4,12,5,128]{3,0,2,1:T(4,128)S(1)} async-done(((f32[4,12,5,128]{3,0,2,1:T(4,128)}), f32[4,12,5,128]{3,0,2,1:T(4,128)S(1)}, u32[]{:S(2)}, u32[]{:S(2)}) %all-to-all-start) | async-done | bytes 122912 | tf_op jit(solution)/shard_map/all_to_all | solution.py:157
  30.7 0.2 multiply_subtract_fusion.7
  30.9 0.2 slice_bitcast_fusion.1
  31.1 0.3 fusion.58
  31.4 0.3 fusion.50
  31.7 0.2 subtract_bitcast_fusion
  31.9 0.3 fusion.39
  32.3 1.5 %fusion.23 = f32[48,256,64]{1,2,0:T(8,128)S(1)} fusion(f32[48,128,1,32]{1,3,2,0:T(8,128)S(1)} %get-tuple-element.32, f32[48,128,1,32]{1,3,2,0:T(8,128)S(1)} %get-tuple-element.31, f32[48,128,1,32]{1,3,2,0:T(8,128)S(1)} %get-tuple-element.30, f32[48,128,1,32]{1,3,2,0:T(8,128)S(1)} %get-tuple-element.29, f32[1,32,64]{2,1,0:T(8,128)S(1)} %get-tuple-element.63, ...), kind=kOutput, calls=%fused_computation.20 | convolution fusion | flops 304353280 | bytes 6307840 | tf_op jit(solution)/shard_map/ikcx,cxn->ikn/dot_general | solution.py:71
  33.8 0.4 fusion.121
  34.2 0.1 slice.100
  34.4 1.5 %multiply_convert_fusion = bf16[48,32,64]{2,1,0:T(8,128)(2,1)S(1)} fusion(f32[48,128,32]{1,2,0:T(8,128)S(1)} %get-tuple-element.22, f32[48,128,32]{1,2,0:T(8,128)S(1)} %get-tuple-element.23, f32[48,128,64]{1,2,0:T(8,128)S(1)} %slice.100, f32[48,128,32]{1,2,0:T(8,128)S(1)} %get-tuple-element.24, f32[48,128,32]{1,2,0:T(8,128)S(1)} %get-tuple-element.21), kind=kOutput, calls=%fused_computation.47 | convolution fusion | flops 153157632 | bytes 4915200 | tf_op jit(solution)/shard_map/ikp,ikn->ipn/dot_general | solution.py:77
  35.9 0.4 convert_element_type.164
  36.2 0.1 convert_reduce_fusion.2
  36.5 0.2 select_reduce_fusion
  36.7 0.3 convolution_convert_fusion
  37.0 1.0 all_to_all.25
  38.0 12.7 %all-to-all-start.1 = ((bf16[64,2,2176]{2,1,0:T(2,128)(2,1)}), bf16[64,2,2176]{2,1,0:T(2,128)(2,1)S(1)}, u32[]{:S(2)}, u32[]{:S(2)}) async-start(bf16[64,2,2176]{2,1,0:T(2,128)(2,1)} %all_to_all.25), calls=%async_computation.1 | async-start | bytes 1114112 | tf_op jit(solution)/shard_map/all_to_all | solution.py:168
  50.8 0.1 fusion.108
  50.9 0.1 fusion.102
  51.0 0.1 fusion.104
  51.1 0.1 fusion.95
  51.3 17.4 %all-to-all-done.1 = bf16[64,2,2176]{2,1,0:T(2,128)(2,1)S(1)} async-done(((bf16[64,2,2176]{2,1,0:T(2,128)(2,1)}), bf16[64,2,2176]{2,1,0:T(2,128)(2,1)S(1)}, u32[]{:S(2)}, u32[]{:S(2)}) %all-to-all-start.1) | async-done | bytes 557088 | tf_op jit(solution)/shard_map/all_to_all | solution.py:168
  68.7 0.2 all_to_all.27
  69.0 0.2 convert_reduce_fusion
  69.2 0.3 copy.58
  69.5 3.0 %copy.59 = bf16[128,32,2,32]{3,1,2,0:T(8,128)(2,1)S(1)} copy(bf16[128,32,2,32]{0,3,2,1:T(8,128)(2,1)S(1)} %bitcast.255) | data formatting | bytes 1048576 | tf_op jit(solution)/shard_map/reshape | solution.py:169
  72.5 2.1 %fusion.18 = bf16[128,2,32,64]{3,2,1,0:T(8,128)(2,1)} fusion(bf16[128,32,2,32]{3,1,2,0:T(8,128)(2,1)S(1)} %copy.59, s32[128,32]{1,0:T(8,128)S(1)} %iota_add_fusion), kind=kOutput, calls=%fused_computation.19 | convolution fusion | flops 34340864 | bytes 1589248 | tf_op jit(solution)/shard_map/scpq,sqw->scpw/dot_general | solution.py:92
  74.6 3.2 %copy.75 = bf16[128,2,32,64]{0,3,1,2:T(8,128)(2,1)S(1)} copy(bf16[128,2,32,64]{3,2,1,0:T(8,128)(2,1)} %fusion.18) | data formatting | bytes 2097152 | tf_op jit(solution)/shard_map/reshape | solution.py:95
  77.8 0.4 convolution_bitcast_fusion.3
  78.2 0.6 convolution_bitcast_fusion.2
  78.9 0.2 multiply_subtract_fusion.2
  79.0 0.6 fusion.30
  79.7 0.9 copy.63
  80.6 1.0 reshape.890
  81.6 18.0 %all_to_all.32 = bf16[64,2,1024]{2,1,0:T(2,128)(2,1)S(1)} all-to-all(bf16[64,2,1024]{2,1,0:T(2,128)(2,1)S(1)} %reshape.890), channel_id=1, replica_groups=mesh['chan'=12,'tile'=64] {'tile'}, dimensions={0} | all-to-all | bytes 524288 | tf_op jit(solution)/shard_map/all_to_all | solution.py:175
  99.6 0.3 copy.64
  99.9 0.5 convolution_bitcast_fusion
  100.4 0.2 multiply_subtract_fusion.1
  100.6 0.4 fusion.32
  101.0 0.9 div.37
  (21 shorter events, 0.6 us)
Async XLA Ops:
  4.5 26.1 %all-to-all-start = ((f32[4,12,5,128]{3,0,2,1:T(4,128)}), f32[4,12,5,128]{3,0,2,1:T(4,128)S(1)}, u32[]{:S(2)}, u32[]{:S(2)}) async-start(f32[4,12,5,128]{3,0,2,1:T(4,128)} %pad_maximum_fusion.1), calls=%async_computation | async-start | bytes 245760 | tf_op jit(solution)/shard_map/all_to_all | solution.py:157
  38.0 30.7 %all-to-all-start.1 = ((bf16[64,2,2176]{2,1,0:T(2,128)(2,1)}), bf16[64,2,2176]{2,1,0:T(2,128)(2,1)S(1)}, u32[]{:S(2)}, u32[]{:S(2)}) async-start(bf16[64,2,2176]{2,1,0:T(2,128)(2,1)} %all_to_all.25), calls=%async_computation.1 | async-start | bytes 1114112 | tf_op jit(solution)/shard_map/all_to_all | solution.py:168

commit v9 on v8

--- a/solution.py
+++ b/solution.py
@@ -150,15 +150,19 @@
     masked = samples[0] * live_mask[:, None, None, None]
     owners = block_owner[0, :, 0]
     cols = placement_map[0, :, 1]
-    meta = jnp.stack([owners, cols // NS, cols % NS], axis=1).astype(jnp.float32)
-    meta = jnp.pad(meta, ((0, 0), (0, steps_time - 3)))
+    meta = jnp.stack([owners, cols], axis=1).astype(jnp.float32)
+    meta = jnp.pad(meta, ((0, 0), (0, steps_time - 2)))
     meta = jnp.broadcast_to(meta[:, None, None, :], (blocks, channels, 1, steps_time))
     payload = jnp.concatenate([masked, uv_coords[0], meta], axis=2)
     arrived = lax.all_to_all(payload, "chan", split_axis=1, concat_axis=0, tiled=True)
     arrived = arrived.reshape(group_blocks, 5, steps_time)
     formed = form_subgrids(arrived[:, 0:2], arrived[:, 2:4])
     cell_count = 2 * NS * NS
-    group_meta = arrived[:, 4, 0:META].astype(jnp.bfloat16)
+    group_cols = arrived[:, 4, 1]
+    col_hi = jnp.floor(group_cols / NS)
+    col_lo = group_cols - NS * col_hi
+    group_meta = jnp.stack([arrived[:, 4, 0], col_hi, col_lo], axis=1)
+    group_meta = jnp.pad(group_meta, ((0, 0), (0, META - 3))).astype(jnp.bfloat16)
     arrived = jnp.concatenate([formed.reshape(group_blocks, cell_count), group_meta], axis=1)
     group_owners = group_meta[:, 0].astype(jnp.int32)
     target = slot_targets(group_owners, tile_count, capacity)

time: 102 us -> 103 us (level)
  no operation moved by 1% of the time
where the time goes in v9:
time: 103 us; the launch traced here: 102 us
  starting transfers between devices  28.4 us (28%)
  waiting for transfers between devices  27.6 us (27%)
  blocking collectives  18 us (17%)
  local copies, waits for them, and re-layouts  13.3 us (13%)
  matrix products  7.9 us (8%)
  other arithmetic  6.11 us (6%)
    all_to_all x1, blocking collectives, per_device(): lax.all_to_all(half, 'tile', split_axis=0, concat_axis=0, tiled=True)  18 us
    all_to_all x1, waiting for transfers between devices, per_device(): lax.all_to_all(outgoing, 'tile', split_axis=0, concat_axis=0, tiled=True)  17.4 us
    all_to_all x1, starting transfers between devices, per_device(): lax.all_to_all(payload, 'chan', split_axis=1, concat_axis=0, tiled=True)  15.7 us
    all_to_all x1, starting transfers between devices, per_device(): lax.all_to_all(outgoing, 'tile', split_axis=0, concat_axis=0, tiled=True)  12.7 us
    all_to_all x1, waiting for transfers between devices, per_device(): lax.all_to_all(payload, 'chan', split_axis=1, concat_axis=0, tiled=True)  10.1 us
    reshape x1, local copies, waits for them, and re-layouts, place_windows(): shifted = shifted.reshape(slots, 2, NS, 2, NS)  3.2 us
    reshape x1, local copies, waits for them, and re-layouts, per_device(): incoming[:, :cell_count].reshape(slot_count, NS, 2, NS)  2.98 us
  transfers between devices with their start and end apart: 2, of which 2 were waited for; matrix products, arithmetic and copies ran while one was open for 1% of the time, Pallas kernels for 0%

profile of v9, /device:TPU:1, one launch (start us, length us, event | category | flops | bytes accessed | tf_op | source)
XLA Modules:
  0.0 102.3 jit_solution(6345345421226095237)
XLA Ops:
  0.7 0.8 copy.87
  1.5 0.7 slice_bitcast_fusion.2
  2.2 0.7 add_convert_fusion
  2.8 0.1 copy.79
  2.9 0.9 bitcast_multiply_fusion.4
  3.8 0.7 pad_maximum_fusion.1
  4.5 15.7 %all-to-all-start = ((f32[4,12,5,128]{3,0,2,1:T(4,128)}), f32[4,12,5,128]{3,0,2,1:T(4,128)S(1)}, u32[]{:S(2)}, u32[]{:S(2)}) async-start(f32[4,12,5,128]{3,0,2,1:T(4,128)} %pad_maximum_fusion.1), calls=%async_computation | async-start | bytes 245760 | tf_op jit(solution)/shard_map/all_to_all | solution.py:157
  20.5 10.1 %all-to-all-done = f32[4,12,5,128]{3,0,2,1:T(4,128)S(1)} async-done(((f32[4,12,5,128]{3,0,2,1:T(4,128)}), f32[4,12,5,128]{3,0,2,1:T(4,128)S(1)}, u32[]{:S(2)}, u32[]{:S(2)}) %all-to-all-start) | async-done | bytes 122912 | tf_op jit(solution)/shard_map/all_to_all | solution.py:157
  30.6 0.2 multiply_subtract_fusion.7
  30.9 0.2 slice_bitcast_fusion.1
  31.1 0.3 fusion.62
  31.4 0.3 fusion.53
  31.7 0.2 subtract_bitcast_fusion
  31.9 0.3 fusion.39
  32.3 1.5 %fusion.23 = f32[48,256,64]{1,2,0:T(8,128)S(1)} fusion(f32[48,128,1,32]{1,3,2,0:T(8,128)S(1)} %get-tuple-element.28, f32[48,128,1,32]{1,3,2,0:T(8,128)S(1)} %get-tuple-element.27, f32[48,128,1,32]{1,3,2,0:T(8,128)S(1)} %get-tuple-element.26, f32[48,128,1,32]{1,3,2,0:T(8,128)S(1)} %get-tuple-element.25, f32[1,32,64]{2,1,0:T(8,128)S(1)} %get-tuple-element.59, ...), kind=kOutput, calls=%fused_computation.20 | convolution fusion | flops 304353280 | bytes 6307840 | tf_op jit(solution)/shard_map/ikcx,cxn->ikn/dot_general | solution.py:71
  33.8 0.4 fusion.129
  34.2 0.1 slice.101
  34.3 0.1 convert_reduce_fusion.2
  34.5 0.1 fusion.114
  34.6 0.2 slice_reduce_fusion
  34.8 1.5 %multiply_convert_fusion = bf16[48,32,64]{2,1,0:T(8,128)(2,1)S(1)} fusion(f32[48,128,32]{1,2,0:T(8,128)S(1)} %get-tuple-element.18, f32[48,128,32]{1,2,0:T(8,128)S(1)} %get-tuple-element.19, f32[48,128,64]{1,2,0:T(8,128)S(1)} %slice.101, f32[48,128,32]{1,2,0:T(8,128)S(1)} %get-tuple-element.20, f32[48,128,32]{1,2,0:T(8,128)S(1)} %get-tuple-element.17), kind=kOutput, calls=%fused_computation.47 | convolution fusion | flops 153157632 | bytes 4915200 | tf_op jit(solution)/shard_map/ikp,ikn->ipn/dot_general | solution.py:77
  36.2 0.4 convert_element_type.162
  36.8 0.2 select_reduce_fusion
  37.0 0.1 copy.80
  37.1 0.3 convolution_convert_fusion
  37.4 1.0 all_to_all.25
  38.4 12.7 %all-to-all-start.1 = ((bf16[64,2,2176]{2,1,0:T(2,128)(2,1)}), bf16[64,2,2176]{2,1,0:T(2,128)(2,1)S(1)}, u32[]{:S(2)}, u32[]{:S(2)}) async-start(bf16[64,2,2176]{2,1,0:T(2,128)(2,1)} %all_to_all.25), calls=%async_computation.1 | async-start | bytes 1114112 | tf_op jit(solution)/shard_map/all_to_all | solution.py:172
  51.2 0.1 fusion.105
  51.5 0.1 fusion.98
  51.7 17.4 %all-to-all-done.1 = bf16[64,2,2176]{2,1,0:T(2,128)(2,1)S(1)} async-done(((bf16[64,2,2176]{2,1,0:T(2,128)(2,1)}), bf16[64,2,2176]{2,1,0:T(2,128)(2,1)S(1)}, u32[]{:S(2)}, u32[]{:S(2)}) %all-to-all-start.1) | async-done | bytes 557088 | tf_op jit(solution)/shard_map/all_to_all | solution.py:172
  69.1 0.2 all_to_all.27
  69.4 0.2 convert_reduce_fusion
  69.6 0.3 copy.61
  69.8 3.0 %copy.62 = bf16[128,32,2,32]{3,1,2,0:T(8,128)(2,1)S(1)} copy(bf16[128,32,2,32]{0,3,2,1:T(8,128)(2,1)S(1)} %bitcast.258) | data formatting | bytes 1048576 | tf_op jit(solution)/shard_map/reshape | solution.py:173
  72.9 2.0 %fusion.18 = bf16[128,2,32,64]{3,2,1,0:T(8,128)(2,1)} fusion(bf16[128,32,2,32]{3,1,2,0:T(8,128)(2,1)S(1)} %copy.62, s32[128,32]{1,0:T(8,128)S(1)} %iota_add_fusion), kind=kOutput, calls=%fused_computation.19 | convolution fusion | flops 34340864 | bytes 1589248 | tf_op jit(solution)/shard_map/scpq,sqw->scpw/dot_general | solution.py:92
  75.0 3.2 %copy.78 = bf16[128,2,32,64]{0,3,1,2:T(8,128)(2,1)S(1)} copy(bf16[128,2,32,64]{3,2,1,0:T(8,128)(2,1)} %fusion.18) | data formatting | bytes 2097152 | tf_op jit(solution)/shard_map/reshape | solution.py:95
  78.2 0.4 convolution_bitcast_fusion.3
  78.6 0.6 convolution_bitcast_fusion.2
  79.2 0.2 multiply_subtract_fusion.2
  79.4 0.6 fusion.30
  80.0 0.9 copy.66
  81.0 1.0 reshape.817
  82.0 18.0 %all_to_all.32 = bf16[64,2,1024]{2,1,0:T(2,128)(2,1)S(1)} all-to-all(bf16[64,2,1024]{2,1,0:T(2,128)(2,1)S(1)} %reshape.817), channel_id=1, replica_groups=mesh['chan'=12,'tile'=64] {'tile'}, dimensions={0} | all-to-all | bytes 524288 | tf_op jit(solution)/shard_map/all_to_all | solution.py:179
  100.0 0.3 copy.67
  100.3 0.5 convolution_bitcast_fusion
  100.8 0.2 multiply_subtract_fusion.1
  101.0 0.4 fusion.32
  101.4 0.9 div.25
  (24 shorter events, 0.9 us)
Async XLA Ops:
  4.5 26.1 %all-to-all-start = ((f32[4,12,5,128]{3,0,2,1:T(4,128)}), f32[4,12,5,128]{3,0,2,1:T(4,128)S(1)}, u32[]{:S(2)}, u32[]{:S(2)}) async-start(f32[4,12,5,128]{3,0,2,1:T(4,128)} %pad_maximum_fusion.1), calls=%async_computation | async-start | bytes 245760 | tf_op jit(solution)/shard_map/all_to_all | solution.py:157
  38.4 30.7 %all-to-all-start.1 = ((bf16[64,2,2176]{2,1,0:T(2,128)(2,1)}), bf16[64,2,2176]{2,1,0:T(2,128)(2,1)S(1)}, u32[]{:S(2)}, u32[]{:S(2)}) async-start(bf16[64,2,2176]{2,1,0:T(2,128)(2,1)} %all_to_all.25), calls=%async_computation.1 | async-start | bytes 1114112 | tf_op jit(solution)/shard_map/all_to_all | solution.py:172

commit v10 on v9

--- a/solution.py
+++ b/solution.py
@@ -79,9 +79,11 @@
 
 
 def slot_targets(owners, tile_count, capacity):
-    onehot = (owners[:, None] == jnp.arange(tile_count)[None, :]).astype(jnp.int32)
-    before = jnp.cumsum(onehot, axis=0) - onehot
-    slot_rank = jnp.sum(before * onehot, axis=1)
+    count = owners.shape[0]
+    onehot = (owners[:, None] == jnp.arange(tile_count)[None, :]).astype(jnp.bfloat16)
+    earlier = (jnp.arange(count)[None, :] < jnp.arange(count)[:, None]).astype(jnp.bfloat16)
+    before = jnp.dot(earlier, onehot, preferred_element_type=jnp.float32)
+    slot_rank = jnp.sum(before * onehot.astype(jnp.float32), axis=1).astype(jnp.int32)
     return owners * capacity + slot_rank
 
 

time: 103 us -> 103 us (level)
  no operation moved by 1% of the time
where the time goes in v10:
time: 103 us; the launch traced here: 102 us
  starting transfers between devices  28.4 us (28%)
  waiting for transfers between devices  27.6 us (27%)
  blocking collectives  18 us (17%)
  local copies, waits for them, and re-layouts  13.3 us (13%)
  matrix products  8.21 us (8%)
  other arithmetic  5.78 us (6%)
    all_to_all x1, blocking collectives, per_device(): lax.all_to_all(half, 'tile', split_axis=0, concat_axis=0, tiled=True)  18 us
    all_to_all x1, waiting for transfers between devices, per_device(): lax.all_to_all(outgoing, 'tile', split_axis=0, concat_axis=0, tiled=True)  17.4 us
    all_to_all x1, starting transfers between devices, per_device(): lax.all_to_all(payload, 'chan', split_axis=1, concat_axis=0, tiled=True)  15.7 us
    all_to_all x1, starting transfers between devices, per_device(): lax.all_to_all(outgoing, 'tile', split_axis=0, concat_axis=0, tiled=True)  12.7 us
    all_to_all x1, waiting for transfers between devices, per_device(): lax.all_to_all(payload, 'chan', split_axis=1, concat_axis=0, tiled=True)  10.1 us
    reshape x1, local copies, waits for them, and re-layouts, place_windows(): shifted = shifted.reshape(slots, 2, NS, 2, NS)  3.2 us
    reshape x1, local copies, waits for them, and re-layouts, per_device(): incoming[:, :cell_count].reshape(slot_count, NS, 2, NS)  2.98 us
  transfers between devices with their start and end apart: 2, of which 2 were waited for; matrix products, arithmetic and copies ran while one was open for 1% of the time, Pallas kernels for 0%

profile of v10, /device:TPU:1, one launch (start us, length us, event | category | flops | bytes accessed | tf_op | source)
XLA Modules:
  0.0 102.3 jit_solution(1328412344115044142)
XLA Ops:
  0.7 0.8 copy.87
  1.5 0.7 slice_bitcast_fusion.2
  2.2 0.7 add_convert_fusion
  2.8 0.1 copy.79
  2.9 0.9 bitcast_multiply_fusion.4
  3.8 0.7 pad_maximum_fusion.1
  4.5 15.7 %all-to-all-start = ((f32[4,12,5,128]{3,0,2,1:T(4,128)}), f32[4,12,5,128]{3,0,2,1:T(4,128)S(1)}, u32[]{:S(2)}, u32[]{:S(2)}) async-start(f32[4,12,5,128]{3,0,2,1:T(4,128)} %pad_maximum_fusion.1), calls=%async_computation | async-start | bytes 245760 | tf_op jit(solution)/shard_map/all_to_all | solution.py:159
  20.5 10.1 %all-to-all-done = f32[4,12,5,128]{3,0,2,1:T(4,128)S(1)} async-done(((f32[4,12,5,128]{3,0,2,1:T(4,128)}), f32[4,12,5,128]{3,0,2,1:T(4,128)S(1)}, u32[]{:S(2)}, u32[]{:S(2)}) %all-to-all-start) | async-done | bytes 122912 | tf_op jit(solution)/shard_map/all_to_all | solution.py:159
  30.6 0.2 multiply_subtract_fusion.7
  30.9 0.2 slice_bitcast_fusion.1
  31.1 0.3 fusion.63
  31.4 0.3 fusion.54
  31.7 0.2 subtract_bitcast_fusion
  31.9 0.3 fusion.40
  32.3 1.5 %fusion.23 = f32[48,256,64]{1,2,0:T(8,128)S(1)} fusion(f32[48,128,1,32]{1,3,2,0:T(8,128)S(1)} %get-tuple-element.28, f32[48,128,1,32]{1,3,2,0:T(8,128)S(1)} %get-tuple-element.27, f32[48,128,1,32]{1,3,2,0:T(8,128)S(1)} %get-tuple-element.26, f32[48,128,1,32]{1,3,2,0:T(8,128)S(1)} %get-tuple-element.25, f32[1,32,64]{2,1,0:T(8,128)S(1)} %get-tuple-element.59, ...), kind=kOutput, calls=%fused_computation.20 | convolution fusion | flops 304353280 | bytes 6307840 | tf_op jit(solution)/shard_map/ikcx,cxn->ikn/dot_general | solution.py:71
  33.8 0.4 fusion.131
  34.2 0.1 slice.101
  34.3 0.2 slice_reduce_fusion
  34.5 0.1 fusion.116
  34.6 0.1 convert_reduce_fusion.2
  34.8 1.5 %multiply_convert_fusion = bf16[48,32,64]{2,1,0:T(8,128)(2,1)S(1)} fusion(f32[48,128,32]{1,2,0:T(8,128)S(1)} %get-tuple-element.18, f32[48,128,32]{1,2,0:T(8,128)S(1)} %get-tuple-element.19, f32[48,128,64]{1,2,0:T(8,128)S(1)} %slice.101, f32[48,128,32]{1,2,0:T(8,128)S(1)} %get-tuple-element.20, f32[48,128,32]{1,2,0:T(8,128)S(1)} %get-tuple-element.17), kind=kOutput, calls=%fused_computation.49 | convolution fusion | flops 153157632 | bytes 4915200 | tf_op jit(solution)/shard_map/ikp,ikn->ipn/dot_general | solution.py:77
  36.2 0.4 convert_element_type.175
  36.6 0.1 copy.80
  36.7 0.3 fusion.33
  37.1 0.3 convolution_convert_fusion
  37.4 1.0 all_to_all.25
  38.4 12.7 %all-to-all-start.1 = ((bf16[64,2,2176]{2,1,0:T(2,128)(2,1)}), bf16[64,2,2176]{2,1,0:T(2,128)(2,1)S(1)}, u32[]{:S(2)}, u32[]{:S(2)}) async-start(bf16[64,2,2176]{2,1,0:T(2,128)(2,1)} %all_to_all.25), calls=%async_computation.1 | async-start | bytes 1114112 | tf_op jit(solution)/shard_map/all_to_all | solution.py:174
  51.1 0.1 fusion.106
  51.5 0.1 fusion.99
  51.6 17.4 %all-to-all-done.1 = bf16[64,2,2176]{2,1,0:T(2,128)(2,1)S(1)} async-done(((bf16[64,2,2176]{2,1,0:T(2,128)(2,1)}), bf16[64,2,2176]{2,1,0:T(2,128)(2,1)S(1)}, u32[]{:S(2)}, u32[]{:S(2)}) %all-to-all-start.1) | async-done | bytes 557088 | tf_op jit(solution)/shard_map/all_to_all | solution.py:174
  69.1 0.2 all_to_all.27
  69.4 0.2 convert_reduce_fusion
  69.5 0.3 copy.61
  69.8 3.0 %copy.62 = bf16[128,32,2,32]{3,1,2,0:T(8,128)(2,1)S(1)} copy(bf16[128,32,2,32]{0,3,2,1:T(8,128)(2,1)S(1)} %bitcast.258) | data formatting | bytes 1048576 | tf_op jit(solution)/shard_map/reshape | solution.py:175
  72.9 2.1 %fusion.18 = bf16[128,2,32,64]{3,2,1,0:T(8,128)(2,1)} fusion(bf16[128,32,2,32]{3,1,2,0:T(8,128)(2,1)S(1)} %copy.62, s32[128,32]{1,0:T(8,128)S(1)} %iota_add_fusion), kind=kOutput, calls=%fused_computation.19 | convolution fusion | flops 34340864 | bytes 1589248 | tf_op jit(solution)/shard_map/scpq,sqw->scpw/dot_general | solution.py:94
  75.0 3.2 %copy.78 = bf16[128,2,32,64]{0,3,1,2:T(8,128)(2,1)S(1)} copy(bf16[128,2,32,64]{3,2,1,0:T(8,128)(2,1)} %fusion.18) | data formatting | bytes 2097152 | tf_op jit(solution)/shard_map/reshape | solution.py:97
  78.2 0.4 convolution_bitcast_fusion.3
  78.6 0.6 convolution_bitcast_fusion.2
  79.2 0.2 multiply_subtract_fusion.2
  79.4 0.6 fusion.30
  80.0 0.9 copy.66
  81.0 1.0 reshape.818
  82.0 18.0 %all_to_all.32 = bf16[64,2,1024]{2,1,0:T(2,128)(2,1)S(1)} all-to-all(bf16[64,2,1024]{2,1,0:T(2,128)(2,1)S(1)} %reshape.818), channel_id=1, replica_groups=mesh['chan'=12,'tile'=64] {'tile'}, dimensions={0} | all-to-all | bytes 524288 | tf_op jit(solution)/shard_map/all_to_all | solution.py:181
  100.0 0.3 copy.67
  100.3 0.5 convolution_bitcast_fusion
  100.8 0.2 multiply_subtract_fusion.1
  101.0 0.4 fusion.32
  101.4 0.9 div.25
  (22 shorter events, 0.8 us)
Async XLA Ops:
  4.5 26.1 %all-to-all-start = ((f32[4,12,5,128]{3,0,2,1:T(4,128)}), f32[4,12,5,128]{3,0,2,1:T(4,128)S(1)}, u32[]{:S(2)}, u32[]{:S(2)}) async-start(f32[4,12,5,128]{3,0,2,1:T(4,128)} %pad_maximum_fusion.1), calls=%async_computation | async-start | bytes 245760 | tf_op jit(solution)/shard_map/all_to_all | solution.py:159
  38.4 30.7 %all-to-all-start.1 = ((bf16[64,2,2176]{2,1,0:T(2,128)(2,1)}), bf16[64,2,2176]{2,1,0:T(2,128)(2,1)S(1)}, u32[]{:S(2)}, u32[]{:S(2)}) async-start(bf16[64,2,2176]{2,1,0:T(2,128)(2,1)} %all_to_all.25), calls=%async_computation.1 | async-start | bytes 1114112 | tf_op jit(solution)/shard_map/all_to_all | solution.py:174
